TPU v7x, 256 devices: a whole 4x4x8 slice. The times are simulated.
256 devices in a mesh: row: 4 (over y), col: 4 (over x), dp: 16 (over z, core).
Axes of the slice: x: 4, y: 4, z: 8, core: 2. Of those that a mesh axis runs over, the one named last changes fastest.
Arguments:
- hidden_states: bfloat16 [16384, 1536], P(('dp', 'row'), 'col'), may hold values from -18 to 18
- w_query: bfloat16 [1536, 1536], P('col', 'row'), may hold values from -0.102062073 to 0.102062073
- w_key_value: bfloat16 [1536, 512], P('col'), may hold values from -0.102062073 to 0.102062073
- adapter_down: bfloat16 [1024, 1536, 16], P('dp', 'col'), may hold values from -0.15625 to 0.15625
- adapter_up: bfloat16 [1024, 16, 1536], P('dp', None, 'row'), may hold values from -1.5 to 1.5
- req_lengths: int32 [16, 8], replicated, may hold values from 1 to 160, 960 in all within a row
- req_adapter: int32 [16, 8], replicated, may hold values from 0 to 1023, as said below
Outputs:
- attention: bfloat16 [16384, 1536], P(('dp', 'col'), 'row')
- kv_cache: bfloat16 [16384, 512], P(('dp', 'col'))
Inputs may be any that keep to these rules, and one draw needn't show every extreme that they name: `req_lengths`: the lengths of one block sum to 960, and each block has a request of exactly 160 tokens. `req_adapter`: adapters k * 64 to (k + 1) * 64 - 1 are those of index k of dp; the requests of one block use adapters of one index of dp at most 1 times, and some index of dp is used exactly that often by every block.
All inputs are finite; a program needn't handle non-finite values.
Results may differ from a plain program's by a relative error of at most 0.0072.
Values may be sent and summed in bfloat16 or wider, within the bound.
No kernel may reach another device: no remote copies, remote signals or barrier semaphores. Data moves between devices by JAX's collectives and lax.ppermute only.
A program may use at most 128 MiB of HBM per device.

v0:
```python
import math

import jax
import jax.numpy as jnp
from jax import lax
from jax.sharding import PartitionSpec as P


HEAD_DIM = 128


masked_score = -1e30


def block_layout(lengths_row, block_len):
    prefix_len = block_len - jnp.sum(lengths_row)
    ends_at = jnp.cumsum(lengths_row) + prefix_len
    starts = ends_at - lengths_row
    positions = jnp.arange(block_len, dtype=jnp.int32)
    segment = jnp.sum((positions[:, None] >= starts[None, :]).astype(jnp.int32), axis=1)
    return (starts, segment, positions)


def make_attend(query_rows, segment, first_row, kv_group, head_size, kv_half):
    own_rows = query_rows.shape[0]
    heads_here = query_rows.shape[1] // head_size
    query_heads = query_rows.reshape(own_rows, heads_here, head_size)
    query_pos = first_row + jnp.arange(own_rows, dtype=jnp.int32)
    query_seg = lax.dynamic_slice_in_dim(segment, first_row, own_rows, 0)
    score_scale = 1.0 / math.sqrt(head_size)

    def attend(state_in, key_block, key_start):
        running_max, running_sum, running_out = state_in
        block_size = key_block.shape[0]
        key_rows = lax.dynamic_slice_in_dim(key_block, kv_group * head_size, head_size, 1)
        values = lax.dynamic_slice_in_dim(key_block, kv_half + kv_group * head_size, head_size, 1)
        key_pos = jnp.arange(block_size, dtype=jnp.int32)
        allowed = (key_pos[None, :] <= query_pos[:, None]) & (
            (segment[None, :] == query_seg[:, None]) | (segment[None, :] == 0)
        )
        scores = (
            jnp.einsum("qhd,kd->hqk", query_heads, key_rows, preferred_element_type=jnp.float32)
            * score_scale
        )
        scores = jnp.where(allowed[None], scores, masked_score)
        new_max = jnp.maximum(running_max, jnp.max(scores, axis=2))
        weights = jnp.where(allowed[None], jnp.exp(scores - new_max[:, :, None]), 0.0)
        running_sum = jnp.sum(weights, axis=2)
        running_out = jnp.einsum(
            "hqk,kd->hqd", weights.astype(jnp.bfloat16), values, preferred_element_type=jnp.float32
        )
        return (new_max, running_sum, running_out)

    initial = (
        jnp.full((heads_here, own_rows), masked_score, jnp.float32),
        jnp.zeros((heads_here, own_rows), jnp.float32),
        jnp.zeros((heads_here, own_rows, head_size), jnp.float32),
    )
    return (attend, initial)


def shifted_copies(x, axis_name):
    size = lax.axis_size(axis_name)
    copies = [x]
    for shift in range(1, size):
        perm = [(i, (i - shift) % size) for i in range(size)]
        copies.append(lax.ppermute(x, axis_name, perm))
    return copies


def ring_gather(x, axis_name, axis):
    size = lax.axis_size(axis_name)
    me = lax.axis_index(axis_name)
    copies = shifted_copies(x, axis_name)
    doubled = jnp.stack(copies + copies, axis=0)
    ordered = lax.dynamic_slice_in_dim(doubled, size - me, size, 0)
    moved = jnp.moveaxis(ordered, 0, axis)
    shape = list(x.shape)
    shape[axis] = shape[axis] * size
    return moved.reshape(shape)


def ring_reduce_scatter(x, axis_name):
    size = lax.axis_size(axis_name)
    me = lax.axis_index(axis_name)
    chunk = x.shape[0] // size
    total = lax.dynamic_slice_in_dim(x, me * chunk, chunk, 0)
    for shift in range(1, size):
        perm = [(i, (i + shift) % size) for i in range(size)]
        piece = lax.dynamic_slice_in_dim(x, ((me + shift) % size) * chunk, chunk, 0)
        total = total + lax.ppermute(piece, axis_name, perm)
    return total


def body(hidden_states, w_query, w_key_value, adapter_down, adapter_up, req_lengths, req_adapter):
    dp_size = lax.axis_size("dp")
    block_index = lax.axis_index("dp")
    col_index = lax.axis_index("col")
    row_index = lax.axis_index("row")
    gathered = ring_gather(hidden_states, "row", 0)
    block_len = gathered.shape[0]
    query_cols = w_query.shape[1]
    kv_cols = w_key_value.shape[1]
    kv_half = kv_cols // 2
    head_size = HEAD_DIM
    heads_here = query_cols // head_size
    heads_total = heads_here * lax.axis_size("row")
    kv_heads = kv_half // head_size
    kv_group = row_index * heads_here // (heads_total // kv_heads)
    own_rows = block_len // lax.axis_size("col")
    first_row = col_index * own_rows
    held_sets = adapter_down.shape[0]
    width_here = adapter_down.shape[1]
    rank_size = adapter_down.shape[2]
    lengths_row = req_lengths[block_index]
    adapters_row = req_adapter[block_index]
    requests = lengths_row.shape[0]
    _, segment, _ = block_layout(lengths_row, block_len)
    request_of = jnp.clip(segment - 1, 0, requests - 1)
    holders = adapters_row // held_sets
    wanted_from_me = (req_adapter // held_sets) == block_index
    local_pick = jnp.sum(jnp.where(wanted_from_me, req_adapter % held_sets, 0), axis=1)
    down_pick = jnp.transpose(jnp.take(adapter_down, local_pick, axis=0), (0, 2, 1))
    up_pick = jnp.take(adapter_up, local_pick, axis=0)
    outgoing = jnp.concatenate([down_pick, up_pick], axis=1)
    incoming = lax.all_to_all(outgoing, "dp", split_axis=0, concat_axis=0, tiled=True)
    flat_down = incoming[:, :rank_size, :].reshape(dp_size * rank_size, width_here).T
    flat_up = incoming[:, rank_size:, :].reshape(dp_size * rank_size, query_cols).astype(jnp.float32)
    reduced = jnp.dot(gathered, flat_down, preferred_element_type=jnp.float32)
    request_ids = jnp.arange(requests, dtype=jnp.int32)
    token_holder = jnp.sum(
        jnp.where(segment[:, None] == request_ids[None, :] + 1, holders[None, :] + 1, 0), axis=1
    ) - 1
    slot_ids = jnp.arange(dp_size, dtype=jnp.int32)
    token_mask = slot_ids[None, :] == token_holder[:, None]
    reduced = reduced.reshape(block_len, dp_size, rank_size)
    low_partial = jnp.sum(jnp.where(token_mask[:, :, None], reduced, 0.0), axis=1)
    low_rank = ring_reduce_scatter(low_partial, "col")
    own_mask = lax.dynamic_slice_in_dim(token_mask, first_row, own_rows, 0)
    spread = jnp.where(own_mask[:, :, None], low_rank[:, None, :], 0.0)
    spread = spread.reshape(own_rows, dp_size * rank_size)
    adapter_term = jnp.dot(spread, flat_up, precision=lax.Precision.HIGHEST)
    key_cols = lax.dynamic_slice_in_dim(w_key_value, kv_group * head_size, head_size, 1)
    value_cols = lax.dynamic_slice_in_dim(w_key_value, kv_half + kv_group * head_size, head_size, 1)
    both_weights = jnp.concatenate([w_query, key_cols, value_cols], axis=1)
    partial_value = jnp.dot(gathered, both_weights, preferred_element_type=jnp.float32)
    summed = ring_reduce_scatter(partial_value, "col")
    query_rows = (summed[:, :query_cols] + adapter_term).astype(jnp.bfloat16)
    head_kv = summed[:, query_cols:].astype(jnp.bfloat16)
    row_size = lax.axis_size("row")
    partner = [(i, (i + row_size // kv_heads) % row_size) for i in range(row_size)]
    other_kv = lax.ppermute(head_kv, "row", partner)
    first_is_own = kv_group == 0
    low_head = jnp.where(first_is_own, head_kv, other_kv)
    high_head = jnp.where(first_is_own, other_kv, head_kv)
    kv_cache = jnp.concatenate(
        [low_head[:, :head_size], high_head[:, :head_size], low_head[:, head_size:], high_head[:, head_size:]],
        axis=1,
    )
    attend, initial = make_attend(query_rows, segment, first_row, 0, head_size, head_size)
    _, running_sum, running_out = attend(initial, ring_gather(head_kv, "col", 0), jnp.int32(0))
    attention = (running_out / running_sum[:, :, None]).astype(jnp.bfloat16)
    attention = jnp.transpose(attention, (1, 0, 2)).reshape(own_rows, query_cols)
    return (attention, kv_cache)


def solution(mesh):
    return jax.shard_map(
        body,
        mesh=mesh,
        in_specs=(
            P(("dp", "row"), "col"),
            P("col", "row"),
            P("col", None),
            P("dp", "col", None),
            P("dp", None, "row"),
            P(),
            P(),
        ),
        out_specs=(P(("dp", "col"), "row"), P(("dp", "col"), None)),
        check_vma=False,
    )
```

profile of v0, /device:TPU:24, one launch (start us, length us, event | category | flops | bytes accessed | tf_op | source)
XLA Modules:
  0.0 79.6 jit_solution(4485525714544195611)
XLA Ops:
  0.6 0.0 copy-start
  0.6 0.8 %collective-permute-start = (bf16[256,384]{1,0:T(8,128)(2,1)}, bf16[256,384]{1,0:T(8,128)(2,1)S(1)}, u32[]{:S(2)}, u32[]{:S(2)}) collective-permute-start(bf16[256,384]{1,0:T(8,128)(2,1)} %param.7), channel_id=1, source_target_pairs={{0,192},{64,0},{128,64},{192,128},{1,193},{65,1},{129,65},{193,129... | collective-permute-start | bytes 589832 | tf_op jit(solution)/shard_map/ppermute | solution.py:67
  1.5 2.5 %collective-permute-start.2 = (bf16[256,384]{1,0:T(8,128)(2,1)}, bf16[256,384]{1,0:T(8,128)(2,1)S(1)}, u32[]{:S(2)}, u32[]{:S(2)}) collective-permute-start(bf16[256,384]{1,0:T(8,128)(2,1)} %param.7), channel_id=1, source_target_pairs={{0,64},{64,128},{128,192},{192,0},{1,65},{65,129},{129,193},{193,1... | collective-permute-start | bytes 589832 | tf_op jit(solution)/shard_map/ppermute | solution.py:67
  4.0 0.2 collective-permute-start.1
  4.1 0.7 fusion.38
  4.9 0.0 copy-done
  4.9 0.6 gather_fusion.1
  5.5 0.0 copy-start.3
  5.5 0.0 copy-start.4
  5.5 0.0 copy-start.5
  5.5 1.8 %gather_fusion = bf16[16,384,16]{1,2,0:T(8,128)(2,1)S(1)} fusion(bf16[64,384,16]{1,2,0:T(8,128)(2,1)} %param.10, s32[1024]{0:T(1024)S(1)} %pad_clamp_fusion), kind=kCustom, calls=%fused_computation | custom fusion | bytes 393280 | tf_op jit(solution)/shard_map/jit(_take)/gather | solution.py:123
  7.3 0.1 broadcast_select_fusion
  7.4 0.1 select_bitcast_fusion
  7.5 0.8 pad_maximum_fusion
  8.3 8.5 %all-to-all-start = ((bf16[16,32,384]{2,1,0:T(8,128)(2,1)}), bf16[16,32,384]{2,1,0:T(8,128)(2,1)}, u32[]{:S(2)}, u32[]{:S(2)}) async-start(bf16[16,32,384]{2,1,0:T(8,128)(2,1)} %pad_maximum_fusion), calls=%async_computation | async-start | bytes 786432 | tf_op jit(solution)/shard_map/all_to_all | solution.py:126
  16.9 0.0 copy-done.3
  16.9 0.0 copy-done.4
  16.9 0.0 copy-done.5
  16.9 0.7 fusion.48
  18.4 0.1 subtract_reduce_fusion
  18.5 0.1 convert_reduce_fusion
  18.6 0.1 dynamic_slice.55
  18.6 0.1 select_reduce_fusion
  18.8 1.0 %constant_dynamic-slice_fusion.9 = (bf16[384,128]{1,0:T(8,128)(2,1)S(1)}, bf16[384,128]{1,0:T(8,128)(2,1)S(1)}) fusion(bf16[384,512]{1,0:T(8,128)(2,1)} %param.9, s32[]{:T(128)S(6)} %select_n.145, s32[]{:T(128)S(6)} %select_n.146), kind=kLoop, calls=%fused_computation.94 | loop fusion | bytes 393224 | tf_op jit(solution)/shard_map/dynamic_slice | solution.py:143
  19.8 0.0 collective-permute-done
  19.8 0.0 collective-permute-done.1
  19.9 0.0 collective-permute-done.2
  20.1 0.1 constant_dynamic-slice_fusion.10
  20.2 0.0 copy-start.1
  20.2 2.1 %fusion.17 = f32[1024,640]{0,1:T(8,128)S(1)} fusion(bf16[1024,384]{1,0:T(8,128)(2,1)S(1)} %bitcast.76, bf16[384,128]{1,0:T(8,128)(2,1)S(1)} %get-tuple-element.16, bf16[384,128]{1,0:T(8,128)(2,1)S(1)} %get-tuple-element.15, bf16[384,384]{1,0:T(8,128)(2,1)} %param.8), kind=kOutput, calls=%fused_computation.18 | convolution fusion | flops 504791040 | bytes 3899392 | tf_op jit(solution)/shard_map/dot_general | solution.py:146
  22.3 1.4 %constant_dynamic-slice_fusion.7 = (f32[256,640]{0,1:T(8,128)}, f32[256,640]{0,1:T(8,128)}, f32[256,640]{0,1:T(8,128)}) fusion(f32[1024,640]{0,1:T(8,128)S(1)} %fusion.17, s32[]{:T(128)S(6)} %select_n.148, s32[]{:T(128)S(6)} %select_n.152, s32[]{:T(128)S(6)} %select_n.150), kind=kLoop, calls=%fused_computation.92 | loop fusion | bytes 3932172 | tf_op jit(solution)/shard_map/dynamic_slice | solution.py:90
  23.6 0.0 copy-done.1
  23.6 1.5 %collective-permute-start.3 = (f32[256,640]{0,1:T(8,128)}, f32[256,640]{0,1:T(8,128)}, u32[]{:S(2)}, u32[]{:S(2)}) collective-permute-start(f32[256,640]{0,1:T(8,128)} %get-tuple-element.12), channel_id=1, source_target_pairs={{0,16},{16,32},{32,48},{48,0},{1,17},{17,33},{33,49},{49,1},{2,18}... | collective-permute-start | bytes 1966088 | tf_op jit(solution)/shard_map/ppermute | solution.py:91
  25.1 1.7 %collective-permute-start.5 = (f32[256,640]{0,1:T(8,128)}, f32[256,640]{0,1:T(8,128)}, u32[]{:S(2)}, u32[]{:S(2)}) collective-permute-start(f32[256,640]{0,1:T(8,128)} %get-tuple-element.13), channel_id=1, source_target_pairs={{0,48},{16,0},{32,16},{48,32},{1,49},{17,1},{33,17},{49,33},{2,50}... | collective-permute-start | bytes 1966088 | tf_op jit(solution)/shard_map/ppermute | solution.py:91
  26.9 1.8 %collective-permute-start.4 = (f32[256,640]{0,1:T(8,128)}, f32[256,640]{0,1:T(8,128)}, u32[]{:S(2)}, u32[]{:S(2)}) collective-permute-start(f32[256,640]{0,1:T(8,128)} %get-tuple-element.14), channel_id=1, source_target_pairs={{0,32},{16,48},{32,0},{48,16},{1,33},{17,49},{33,1},{49,17},{2,34}... | collective-permute-start | bytes 1966088 | tf_op jit(solution)/shard_map/ppermute | solution.py:91
  28.7 1.8 %all-to-all-done = bf16[16,32,384]{2,1,0:T(8,128)(2,1)} async-done(((bf16[16,32,384]{2,1,0:T(8,128)(2,1)}), bf16[16,32,384]{2,1,0:T(8,128)(2,1)}, u32[]{:S(2)}, u32[]{:S(2)}) %all-to-all-start) | async-done | bytes 393248 | tf_op jit(solution)/shard_map/all_to_all | solution.py:126
  30.5 1.6 %fusion.6 = f32[1024,16]{0,1:T(8,128)S(1)} fusion(bf16[1024,384,1]{1,0,2:T(8,128)(2,1)} %bitcast.77, pred[1024,16]{0,1:T(8,128)(4,1)S(1)} %iota_compare_fusion.1, bf16[16,32,384]{2,1,0:T(8,128)(2,1)} %all-to-all-done), kind=kOutput, calls=%fused_computation.10 | convolution fusion | flops 201834496 | bytes 1064960 | tf_op jit(solution)/shard_map/dot_general | solution.py:129
  32.1 1.6 %collective-permute-start.9 = (f32[256,16]{0,1:T(8,128)S(1)}, f32[256,16]{0,1:T(8,128)S(1)}, u32[]{:S(2)}, u32[]{:S(2)}) collective-permute-start(f32[256,16]{0,1:T(8,128)S(1)} %get-tuple-element.23), channel_id=1, source_target_pairs={{0,16},{16,32},{32,48},{48,0},{1,17},{17,33},{33,49},{49,1},{2,18}... | collective-permute-start | bytes 49160 | tf_op jit(solution)/shard_map/ppermute | solution.py:91
  33.7 1.4 %fusion.10 = pred[256,1024]{0,1:T(8,128)(4,1)} fusion(s32[256]{0:T(256)S(1)} %dynamic_slice.55, s32[256]{0:T(256)S(1)} %iota_add_fusion, s32[1024]{0:T(1024)S(1)} %convert_reduce_fusion, pred[1024]{0:T(1024)(128)(4,1)S(1)} %broadcast_compare_fusion), kind=kLoop, calls=%fused_computation.14 | loop fusion | flops 1048576 | bytes 269312 | tf_op jit(solution)/shard_map/and | solution.py:38
  35.1 1.7 %collective-permute-start.11 = (f32[256,16]{0,1:T(8,128)S(1)}, f32[256,16]{0,1:T(8,128)}, u32[]{:S(2)}, u32[]{:S(2)}) collective-permute-start(f32[256,16]{0,1:T(8,128)S(1)} %get-tuple-element.24), channel_id=1, source_target_pairs={{0,48},{16,0},{32,16},{48,32},{1,49},{17,1},{33,17},{49,33},{2,50}... | collective-permute-start | bytes 49160 | tf_op jit(solution)/shard_map/ppermute | solution.py:91
  36.9 17.4 %collective-permute-done.9 = f32[256,16]{0,1:T(8,128)S(1)} collective-permute-done((f32[256,16]{0,1:T(8,128)S(1)}, f32[256,16]{0,1:T(8,128)S(1)}, u32[]{:S(2)}, u32[]{:S(2)}) %collective-permute-start.9) | collective-permute-done | bytes 16416 | tf_op jit(solution)/shard_map/ppermute | solution.py:91
  54.2 4.0 %collective-permute-start.10 = (f32[256,16]{0,1:T(8,128)S(1)}, f32[256,16]{0,1:T(8,128)}, u32[]{:S(2)}, u32[]{:S(2)}) collective-permute-start(f32[256,16]{0,1:T(8,128)S(1)} %get-tuple-element.25), channel_id=1, source_target_pairs={{0,32},{16,48},{32,0},{48,16},{1,33},{17,49},{33,1},{49,17},{2,34}... | collective-permute-start | bytes 49160 | tf_op jit(solution)/shard_map/ppermute | solution.py:91
  58.2 0.0 collective-permute-done.11
  58.2 1.8 %collective-permute-done.10 = f32[256,16]{0,1:T(8,128)} collective-permute-done((f32[256,16]{0,1:T(8,128)S(1)}, f32[256,16]{0,1:T(8,128)}, u32[]{:S(2)}, u32[]{:S(2)}) %collective-permute-start.10) | collective-permute-done | bytes 16416 | tf_op jit(solution)/shard_map/ppermute | solution.py:91
  60.0 0.7 add_add_fusion.1
  60.8 0.0 collective-permute-done.3
  60.8 0.0 collective-permute-done.5
  60.8 0.0 collective-permute-done.4
  60.8 1.7 %add_add_fusion = f32[256,640]{0,1:T(8,128)S(1)} fusion(f32[256,640]{0,1:T(8,128)} %collective-permute-done.5, f32[256,640]{0,1:T(8,128)} %collective-permute-done.4, f32[256,640]{0,1:T(8,128)} %collective-permute-done.3, f32[1024,640]{0,1:T(8,128)S(1)} %fusion.17, s32[]{:T(128)S(6)} %select_n.142), kind=kLoop, calls=%fused_computation.17 | loop fusion | flops 491520 | bytes 3276804 | tf_op jit(solution)/shard_map/add | solution.py:91
  62.5 3.6 %collective-permute-start.12 = (bf16[256,256]{0,1:T(8,128)(2,1)S(1)}, bf16[256,256]{0,1:T(8,128)(2,1)S(1)}, u32[]{:S(2)}, u32[]{:S(2)}) collective-permute-start(bf16[256,256]{0,1:T(8,128)(2,1)S(1)} %get-tuple-element.9), channel_id=1, source_target_pairs={{0,128},{64,192},{128,0},{192,64},{1,129},{65,193},{129,1},{193,65... | collective-permute-start | bytes 393224 | tf_op jit(solution)/shard_map/ppermute | solution.py:152
  66.1 2.1 %collective-permute-start.8 = (bf16[256,256]{0,1:T(8,128)(2,1)S(1)}, bf16[256,256]{0,1:T(8,128)(2,1)S(1)}, u32[]{:S(2)}, u32[]{:S(2)}) collective-permute-start(bf16[256,256]{0,1:T(8,128)(2,1)S(1)} %get-tuple-element.9), channel_id=1, source_target_pairs={{0,16},{16,32},{32,48},{48,0},{1,17},{17,33},{33,49},{49,1},{2,18}... | collective-permute-start | bytes 393224 | tf_op jit(solution)/shard_map/ppermute | solution.py:67
  68.2 2.7 %collective-permute-start.7 = (bf16[256,256]{0,1:T(8,128)(2,1)S(1)}, bf16[256,256]{0,1:T(8,128)(2,1)S(1)}, u32[]{:S(2)}, u32[]{:S(2)}) collective-permute-start(bf16[256,256]{0,1:T(8,128)(2,1)S(1)} %get-tuple-element.9), channel_id=1, source_target_pairs={{0,32},{16,48},{32,0},{48,16},{1,33},{17,49},{33,1},{49,17},{2,34}... | collective-permute-start | bytes 393224 | tf_op jit(solution)/shard_map/ppermute | solution.py:67
  70.9 1.4 %collective-permute-start.6 = (bf16[256,256]{0,1:T(8,128)(2,1)S(1)}, bf16[256,256]{0,1:T(8,128)(2,1)S(1)}, u32[]{:S(2)}, u32[]{:S(2)}) collective-permute-start(bf16[256,256]{0,1:T(8,128)(2,1)S(1)} %get-tuple-element.9), channel_id=1, source_target_pairs={{0,48},{16,0},{32,16},{48,32},{1,49},{17,1},{33,17},{49,33},{2,50}... | collective-permute-start | bytes 393224 | tf_op jit(solution)/shard_map/ppermute | solution.py:67
  72.3 1.3 %fusion.23 = bf16[256,384]{0,1:T(8,128)(2,1)S(1)} fusion(f32[256,640]{0,1:T(8,128)S(1)} %add_add_fusion, bf16[16,32,384]{2,1,0:T(8,128)(2,1)} %all-to-all-done, f32[256,16]{0,1:T(8,128)S(1)} %add_add_fusion.1, pred[256,16]{0,1:T(8,128)(4,1)S(1)} %constant_dynamic-slice_fusion.3), kind=kOutput, calls=%fused_computation.25 | convolution fusion | flops 302252032 | bytes 806912 | tf_op jit(solution)/shard_map/dot_general | solution.py:142
  73.6 0.0 collective-permute-done.12
  73.7 0.8 %copy.28 = bf16[256,512]{1,0:T(8,128)(2,1)} copy(bf16[256,512]{0,1:T(8,128)(2,1)S(1)} %pad_maximum_fusion.1) | data formatting | bytes 524288
  74.5 1.3 %collective-permute-done.6 = bf16[256,256]{0,1:T(8,128)(2,1)S(1)} collective-permute-done((bf16[256,256]{0,1:T(8,128)(2,1)S(1)}, bf16[256,256]{0,1:T(8,128)(2,1)S(1)}, u32[]{:S(2)}, u32[]{:S(2)}) %collective-permute-start.6) | collective-permute-done | bytes 131104 | tf_op jit(solution)/shard_map/ppermute | solution.py:67
  75.9 0.0 collective-permute-done.7
  75.9 0.0 collective-permute-done.8
  76.0 0.2 copy.22
  76.3 0.7 fusion
  77.0 0.8 %fusion.1 = f32[3,256]{1,0:T(4,128)S(1)} fusion(f32[1024,256,3]{1,0,2:T(8,128)S(1)} %get-tuple-element.27, f32[3,256]{1,0:T(4,128)S(1)} %broadcast_maximum_fusion, pred[256,1024]{0,1:T(8,128)(4,1)S(1)} %copy-done.2), kind=kLoop, calls=%fused_computation.5 | loop fusion | flops 3931392 | bytes 3414016 | tf_op jit(solution)/shard_map/reduce_sum | solution.py:48
  77.8 1.0 %fusion.14 = bf16[256,3,128]{0,2,1:T(8,128)(2,1)S(1)} fusion(f32[1024,256,3]{1,0,2:T(8,128)S(1)} %get-tuple-element.27, f32[3,256]{1,0:T(4,128)S(1)} %broadcast_maximum_fusion, pred[256,1024]{0,1:T(8,128)(4,1)S(1)} %copy-done.2, bf16[1024,256]{1,0:T(8,128)(2,1)S(1)} %bitcast.79, f32[256,3]{0,1:T(4,128)S(1)} %bitcast.82), kind=kOutput, calls=%fused_computation.16 | convolution fusion | flops 205455360 | bytes 3874816 | tf_op jit(solution)/shard_map/hqk,kd->hqd/dot_general | solution.py:49
  78.8 0.8 %copy.27 = bf16[256,384]{1,0:T(8,128)(2,1)} copy(bf16[256,384]{0,1:T(8,128)(2,1)S(1)} %bitcast.80) | data formatting | bytes 393216
  (34 shorter events, 0.6 us)
Async XLA Ops:
  0.6 4.2 %copy-start = (bf16[64,16,384]{2,1,0:T(8,128)(2,1)S(1)}, bf16[64,16,384]{2,1,0:T(8,128)(2,1)}, u32[]{:S(2)}) copy-start(bf16[64,16,384]{2,1,0:T(8,128)(2,1)} %param.11) | copy-start | bytes 2359300
  0.6 19.1 %collective-permute-start = (bf16[256,384]{1,0:T(8,128)(2,1)}, bf16[256,384]{1,0:T(8,128)(2,1)S(1)}, u32[]{:S(2)}, u32[]{:S(2)}) collective-permute-start(bf16[256,384]{1,0:T(8,128)(2,1)} %param.7), channel_id=1, source_target_pairs={{0,192},{64,0},{128,64},{192,128},{1,193},{65,1},{129,65},{193,129... | collective-permute-start | bytes 589832 | tf_op jit(solution)/shard_map/ppermute | solution.py:67
  1.5 18.4 %collective-permute-start.2 = (bf16[256,384]{1,0:T(8,128)(2,1)}, bf16[256,384]{1,0:T(8,128)(2,1)S(1)}, u32[]{:S(2)}, u32[]{:S(2)}) collective-permute-start(bf16[256,384]{1,0:T(8,128)(2,1)} %param.7), channel_id=1, source_target_pairs={{0,64},{64,128},{128,192},{192,0},{1,65},{65,129},{129,193},{193,1... | collective-permute-start | bytes 589832 | tf_op jit(solution)/shard_map/ppermute | solution.py:67
  4.0 15.9 %collective-permute-start.1 = (bf16[256,384]{1,0:T(8,128)(2,1)}, bf16[256,384]{1,0:T(8,128)(2,1)S(1)}, u32[]{:S(2)}, u32[]{:S(2)}) collective-permute-start(bf16[256,384]{1,0:T(8,128)(2,1)} %param.7), channel_id=1, source_target_pairs={{0,128},{64,192},{128,0},{192,64},{1,129},{65,193},{129,1},{193,65... | collective-permute-start | bytes 589832 | tf_op jit(solution)/shard_map/ppermute | solution.py:67
  5.5 11.4 %copy-start.3 = (bf16[256,384]{1,0:T(8,128)(2,1)S(1)}, bf16[256,384]{1,0:T(8,128)(2,1)}, u32[]{:S(2)}) copy-start(bf16[256,384]{1,0:T(8,128)(2,1)} %param.7) | copy-start | bytes 589828
  5.5 11.4 %copy-start.4 = (s32[16,8]{0,1:T(8,128)S(1)}, s32[16,8]{0,1:T(8,128)}, u32[]{:S(2)}) copy-start(s32[16,8]{0,1:T(8,128)} %param.13) | copy-start | bytes 1540
  5.5 11.4 %copy-start.5 = (s32[16,8]{0,1:T(8,128)S(1)}, s32[16,8]{0,1:T(8,128)}, u32[]{:S(2)}) copy-start(s32[16,8]{0,1:T(8,128)} %param.12) | copy-start | bytes 1540
  8.3 22.2 %all-to-all-start = ((bf16[16,32,384]{2,1,0:T(8,128)(2,1)}), bf16[16,32,384]{2,1,0:T(8,128)(2,1)}, u32[]{:S(2)}, u32[]{:S(2)}) async-start(bf16[16,32,384]{2,1,0:T(8,128)(2,1)} %pad_maximum_fusion), calls=%async_computation | async-start | bytes 786432 | tf_op jit(solution)/shard_map/all_to_all | solution.py:126
  20.2 3.5 %copy-start.1 = (bf16[4,256,384]{2,1,0:T(8,128)(2,1)}, bf16[4,256,384]{2,1,0:T(8,128)(2,1)S(1)}, u32[]{:S(2)}) copy-start(bf16[4,256,384]{2,1,0:T(8,128)(2,1)S(1)} %constant_dynamic-slice_fusion.10) | copy-start | bytes 2359300
  23.6 37.1 %collective-permute-start.3 = (f32[256,640]{0,1:T(8,128)}, f32[256,640]{0,1:T(8,128)}, u32[]{:S(2)}, u32[]{:S(2)}) collective-permute-start(f32[256,640]{0,1:T(8,128)} %get-tuple-element.12), channel_id=1, source_target_pairs={{0,16},{16,32},{32,48},{48,0},{1,17},{17,33},{33,49},{49,1},{2,18}... | collective-permute-start | bytes 1966088 | tf_op jit(solution)/shard_map/ppermute | solution.py:91
  25.1 35.6 %collective-permute-start.5 = (f32[256,640]{0,1:T(8,128)}, f32[256,640]{0,1:T(8,128)}, u32[]{:S(2)}, u32[]{:S(2)}) collective-permute-start(f32[256,640]{0,1:T(8,128)} %get-tuple-element.13), channel_id=1, source_target_pairs={{0,48},{16,0},{32,16},{48,32},{1,49},{17,1},{33,17},{49,33},{2,50}... | collective-permute-start | bytes 1966088 | tf_op jit(solution)/shard_map/ppermute | solution.py:91
  26.9 33.9 %collective-permute-start.4 = (f32[256,640]{0,1:T(8,128)}, f32[256,640]{0,1:T(8,128)}, u32[]{:S(2)}, u32[]{:S(2)}) collective-permute-start(f32[256,640]{0,1:T(8,128)} %get-tuple-element.14), channel_id=1, source_target_pairs={{0,32},{16,48},{32,0},{48,16},{1,33},{17,49},{33,1},{49,17},{2,34}... | collective-permute-start | bytes 1966088 | tf_op jit(solution)/shard_map/ppermute | solution.py:91
  32.1 22.1 %collective-permute-start.9 = (f32[256,16]{0,1:T(8,128)S(1)}, f32[256,16]{0,1:T(8,128)S(1)}, u32[]{:S(2)}, u32[]{:S(2)}) collective-permute-start(f32[256,16]{0,1:T(8,128)S(1)} %get-tuple-element.23), channel_id=1, source_target_pairs={{0,16},{16,32},{32,48},{48,0},{1,17},{17,33},{33,49},{49,1},{2,18}... | collective-permute-start | bytes 49160 | tf_op jit(solution)/shard_map/ppermute | solution.py:91
  35.1 23.1 %collective-permute-start.11 = (f32[256,16]{0,1:T(8,128)S(1)}, f32[256,16]{0,1:T(8,128)}, u32[]{:S(2)}, u32[]{:S(2)}) collective-permute-start(f32[256,16]{0,1:T(8,128)S(1)} %get-tuple-element.24), channel_id=1, source_target_pairs={{0,48},{16,0},{32,16},{48,32},{1,49},{17,1},{33,17},{49,33},{2,50}... | collective-permute-start | bytes 49160 | tf_op jit(solution)/shard_map/ppermute | solution.py:91
  54.2 5.8 %collective-permute-start.10 = (f32[256,16]{0,1:T(8,128)S(1)}, f32[256,16]{0,1:T(8,128)}, u32[]{:S(2)}, u32[]{:S(2)}) collective-permute-start(f32[256,16]{0,1:T(8,128)S(1)} %get-tuple-element.25), channel_id=1, source_target_pairs={{0,32},{16,48},{32,0},{48,16},{1,33},{17,49},{33,1},{49,17},{2,34}... | collective-permute-start | bytes 49160 | tf_op jit(solution)/shard_map/ppermute | solution.py:91
  62.5 11.1 %collective-permute-start.12 = (bf16[256,256]{0,1:T(8,128)(2,1)S(1)}, bf16[256,256]{0,1:T(8,128)(2,1)S(1)}, u32[]{:S(2)}, u32[]{:S(2)}) collective-permute-start(bf16[256,256]{0,1:T(8,128)(2,1)S(1)} %get-tuple-element.9), channel_id=1, source_target_pairs={{0,128},{64,192},{128,0},{192,64},{1,129},{65,193},{129,1},{193,65... | collective-permute-start | bytes 393224 | tf_op jit(solution)/shard_map/ppermute | solution.py:152
  66.1 9.8 %collective-permute-start.8 = (bf16[256,256]{0,1:T(8,128)(2,1)S(1)}, bf16[256,256]{0,1:T(8,128)(2,1)S(1)}, u32[]{:S(2)}, u32[]{:S(2)}) collective-permute-start(bf16[256,256]{0,1:T(8,128)(2,1)S(1)} %get-tuple-element.9), channel_id=1, source_target_pairs={{0,16},{16,32},{32,48},{48,0},{1,17},{17,33},{33,49},{49,1},{2,18}... | collective-permute-start | bytes 393224 | tf_op jit(solution)/shard_map/ppermute | solution.py:67
  68.2 7.7 %collective-permute-start.7 = (bf16[256,256]{0,1:T(8,128)(2,1)S(1)}, bf16[256,256]{0,1:T(8,128)(2,1)S(1)}, u32[]{:S(2)}, u32[]{:S(2)}) collective-permute-start(bf16[256,256]{0,1:T(8,128)(2,1)S(1)} %get-tuple-element.9), channel_id=1, source_target_pairs={{0,32},{16,48},{32,0},{48,16},{1,33},{17,49},{33,1},{49,17},{2,34}... | collective-permute-start | bytes 393224 | tf_op jit(solution)/shard_map/ppermute | solution.py:67
  70.9 5.0 %collective-permute-start.6 = (bf16[256,256]{0,1:T(8,128)(2,1)S(1)}, bf16[256,256]{0,1:T(8,128)(2,1)S(1)}, u32[]{:S(2)}, u32[]{:S(2)}) collective-permute-start(bf16[256,256]{0,1:T(8,128)(2,1)S(1)} %get-tuple-element.9), channel_id=1, source_target_pairs={{0,48},{16,0},{32,16},{48,32},{1,49},{17,1},{33,17},{49,33},{2,50}... | collective-permute-start | bytes 393224 | tf_op jit(solution)/shard_map/ppermute | solution.py:67
  73.7 2.6 %copy-start.2 = (pred[256,1024]{0,1:T(8,128)(4,1)S(1)}, pred[256,1024]{0,1:T(8,128)(4,1)}, u32[]{:S(2)}) copy-start(pred[256,1024]{0,1:T(8,128)(4,1)} %fusion.10) | copy-start | bytes 786436
where the time goes:
time: 80.1 us; the launch traced here: 79.6 us
  starting transfers between devices  34 us (42%)
  waiting for transfers between devices  22.3 us (28%)
  other arithmetic  7.53 us (9%)
  local copies, waits for them, and re-layouts  7.2 us (9%)
  matrix products  6.73 us (8%)
  between operations  1.87 us (2%)
    ppermute x6, waiting for transfers between devices, ring_reduce_scatter(): total = total + lax.ppermute(piece, axis_name, perm)  19.2 us
    ppermute x6, starting transfers between devices, ring_reduce_scatter(): total = total + lax.ppermute(piece, axis_name, perm)  12.3 us
    ppermute x6, starting transfers between devices, shifted_copies(): copies.append(lax.ppermute(x, axis_name, perm))  9.63 us
    all_to_all x1, starting transfers between devices, body(): lax.all_to_all(outgoing, 'dp', split_axis=0, concat_axis=0, tiled=True)  8.48 us
    ppermute x1, starting transfers between devices, body(): other_kv = lax.ppermute(head_kv, 'row', partner)  3.59 us
    add x2, other arithmetic, ring_reduce_scatter(): total = total + lax.ppermute(piece, axis_name, perm)  2.44 us
    dot_general x1, matrix products, body(): jnp.dot(gathered, both_weights, preferred_element_type=jnp.float32)  2.07 us
    unnamed x28, local copies, waits for them, and re-layouts  2.01 us
  transfers between devices with their start and end apart: 14, of which 4 were waited for; matrix products, arithmetic and copies ran while one was open for 20% of the time, Pallas kernels for 0%

commit v1 on v0

--- a/solution.py
+++ b/solution.py
@@ -34,9 +34,15 @@
         block_size = key_block.shape[0]
         key_rows = lax.dynamic_slice_in_dim(key_block, kv_group * head_size, head_size, 1)
         values = lax.dynamic_slice_in_dim(key_block, kv_half + kv_group * head_size, head_size, 1)
-        key_pos = jnp.arange(block_size, dtype=jnp.int32)
+        parts = block_size // own_rows
+        blocks = jnp.arange(block_size, dtype=jnp.int32).reshape(parts, own_rows)
+        blocks = jnp.concatenate([blocks, blocks], axis=0)
+        key_pos = lax.dynamic_slice_in_dim(blocks, key_start, parts, 0).reshape(-1)
+        seg_blocks = segment.reshape(parts, own_rows)
+        seg_blocks = jnp.concatenate([seg_blocks, seg_blocks], axis=0)
+        key_seg = lax.dynamic_slice_in_dim(seg_blocks, key_start, parts, 0).reshape(-1)
         allowed = (key_pos[None, :] <= query_pos[:, None]) & (
-            (segment[None, :] == query_seg[:, None]) | (segment[None, :] == 0)
+            (key_seg[None, :] == query_seg[:, None]) | (key_seg[None, :] == 0)
         )
         scores = (
             jnp.einsum("qhd,kd->hqk", query_heads, key_rows, preferred_element_type=jnp.float32)
@@ -68,26 +74,14 @@
     return copies
 
 
-def ring_gather(x, axis_name, axis):
-    size = lax.axis_size(axis_name)
-    me = lax.axis_index(axis_name)
-    copies = shifted_copies(x, axis_name)
-    doubled = jnp.stack(copies + copies, axis=0)
-    ordered = lax.dynamic_slice_in_dim(doubled, size - me, size, 0)
-    moved = jnp.moveaxis(ordered, 0, axis)
-    shape = list(x.shape)
-    shape[axis] = shape[axis] * size
-    return moved.reshape(shape)
-
-
-def ring_reduce_scatter(x, axis_name):
+def ring_reduce_scatter(x, axis_name, origin=0):
     size = lax.axis_size(axis_name)
     me = lax.axis_index(axis_name)
     chunk = x.shape[0] // size
-    total = lax.dynamic_slice_in_dim(x, me * chunk, chunk, 0)
+    total = lax.dynamic_slice_in_dim(x, ((me - origin) % size) * chunk, chunk, 0)
     for shift in range(1, size):
         perm = [(i, (i + shift) % size) for i in range(size)]
-        piece = lax.dynamic_slice_in_dim(x, ((me + shift) % size) * chunk, chunk, 0)
+        piece = lax.dynamic_slice_in_dim(x, ((me + shift - origin) % size) * chunk, chunk, 0)
         total = total + lax.ppermute(piece, axis_name, perm)
     return total
 
@@ -97,7 +91,7 @@
     block_index = lax.axis_index("dp")
     col_index = lax.axis_index("col")
     row_index = lax.axis_index("row")
-    gathered = ring_gather(hidden_states, "row", 0)
+    gathered = jnp.concatenate(shifted_copies(hidden_states, "row"), axis=0)
     block_len = gathered.shape[0]
     query_cols = w_query.shape[1]
     kv_cols = w_key_value.shape[1]
@@ -133,9 +127,14 @@
     ) - 1
     slot_ids = jnp.arange(dp_size, dtype=jnp.int32)
     token_mask = slot_ids[None, :] == token_holder[:, None]
+    row_size = lax.axis_size("row")
+    holder_blocks = token_holder.reshape(row_size, -1)
+    holder_blocks = jnp.concatenate([holder_blocks, holder_blocks], axis=0)
+    gathered_holder = lax.dynamic_slice_in_dim(holder_blocks, row_index, row_size, 0).reshape(-1)
+    gathered_mask = slot_ids[None, :] == gathered_holder[:, None]
     reduced = reduced.reshape(block_len, dp_size, rank_size)
-    low_partial = jnp.sum(jnp.where(token_mask[:, :, None], reduced, 0.0), axis=1)
-    low_rank = ring_reduce_scatter(low_partial, "col")
+    low_partial = jnp.sum(jnp.where(gathered_mask[:, :, None], reduced, 0.0), axis=1)
+    low_rank = ring_reduce_scatter(low_partial, "col", row_index)
     own_mask = lax.dynamic_slice_in_dim(token_mask, first_row, own_rows, 0)
     spread = jnp.where(own_mask[:, :, None], low_rank[:, None, :], 0.0)
     spread = spread.reshape(own_rows, dp_size * rank_size)
@@ -144,12 +143,12 @@
     value_cols = lax.dynamic_slice_in_dim(w_key_value, kv_half + kv_group * head_size, head_size, 1)
     both_weights = jnp.concatenate([w_query, key_cols, value_cols], axis=1)
     partial_value = jnp.dot(gathered, both_weights, preferred_element_type=jnp.float32)
-    summed = ring_reduce_scatter(partial_value, "col")
+    summed = ring_reduce_scatter(partial_value, "col", row_index)
     query_rows = (summed[:, :query_cols] + adapter_term).astype(jnp.bfloat16)
     head_kv = summed[:, query_cols:].astype(jnp.bfloat16)
-    row_size = lax.axis_size("row")
     partner = [(i, (i + row_size // kv_heads) % row_size) for i in range(row_size)]
     other_kv = lax.ppermute(head_kv, "row", partner)
+    key_values = jnp.concatenate(shifted_copies(head_kv, "col"), axis=0)
     first_is_own = kv_group == 0
     low_head = jnp.where(first_is_own, head_kv, other_kv)
     high_head = jnp.where(first_is_own, other_kv, head_kv)
@@ -158,7 +157,9 @@
         axis=1,
     )
     attend, initial = make_attend(query_rows, segment, first_row, 0, head_size, head_size)
-    _, running_sum, running_out = attend(initial, ring_gather(head_kv, "col", 0), jnp.int32(0))
+    _, running_sum, running_out = attend(
+        initial, key_values, col_index
+    )
     attention = (running_out / running_sum[:, :, None]).astype(jnp.bfloat16)
     attention = jnp.transpose(attention, (1, 0, 2)).reshape(own_rows, query_cols)
     return (attention, kv_cache)

time: 80.1 us -> 82.6 us (1.031)
  the two profiles are of different devices: /device:TPU:24 before, /device:TPU:32 now
where the time goes in v1:
time: 82.6 us; the launch traced here: 82.1 us
  starting transfers between devices  33.2 us (40%)
  waiting for transfers between devices  25.1 us (30%)
  matrix products  7.74 us (9%)
  other arithmetic  7.72 us (9%)
  local copies, waits for them, and re-layouts  6.68 us (8%)
  between operations  1.74 us (2%)
    ppermute x6, waiting for transfers between devices, ring_reduce_scatter(): total = total + lax.ppermute(piece, axis_name, perm)  20.3 us
    ppermute x6, starting transfers between devices, ring_reduce_scatter(): total = total + lax.ppermute(piece, axis_name, perm)  12.3 us
    ppermute x6, starting transfers between devices, shifted_copies(): copies.append(lax.ppermute(x, axis_name, perm))  11.5 us
    all_to_all x1, starting transfers between devices, body(): lax.all_to_all(outgoing, 'dp', split_axis=0, concat_axis=0, tiled=True)  8.59 us
    ppermute x1, waiting for transfers between devices, body(): other_kv = lax.ppermute(head_kv, 'row', partner)  4.42 us
    unnamed x22, local copies, waits for them, and re-layouts  2.67 us
    add x2, other arithmetic, ring_reduce_scatter(): total = total + lax.ppermute(piece, axis_name, perm)  2.42 us
    dot_general x1, matrix products, body(): jnp.dot(gathered, both_weights, preferred_element_type=jnp.float32)  2.09 us
  transfers between devices with their start and end apart: 14, of which 4 were waited for; matrix products, arithmetic and copies ran while one was open for 18% of the time, Pallas kernels for 0%

profile of v1, /device:TPU:32, one launch (start us, length us, event | category | flops | bytes accessed | tf_op | source)
XLA Modules:
  0.0 82.1 jit_solution(8375971583423978504)
XLA Ops:
  0.6 0.0 copy-start
  0.6 0.0 copy-start.3
  0.7 3.3 %collective-permute-start.1 = (bf16[256,384]{1,0:T(8,128)(2,1)}, bf16[256,384]{1,0:T(8,128)(2,1)S(1)}, u32[]{:S(2)}, u32[]{:S(2)}) collective-permute-start(bf16[256,384]{1,0:T(8,128)(2,1)} %param.7), channel_id=1, source_target_pairs={{0,128},{64,192},{128,0},{192,64},{1,129},{65,193},{129,1},{193,65... | collective-permute-start | bytes 589832 | tf_op jit(solution)/shard_map/ppermute | solution.py:73
  3.9 1.1 %collective-permute-start = (bf16[256,384]{1,0:T(8,128)(2,1)}, bf16[256,384]{1,0:T(8,128)(2,1)S(1)}, u32[]{:S(2)}, u32[]{:S(2)}) collective-permute-start(bf16[256,384]{1,0:T(8,128)(2,1)} %param.7), channel_id=1, source_target_pairs={{0,192},{64,0},{128,64},{192,128},{1,193},{65,1},{129,65},{193,129... | collective-permute-start | bytes 589832 | tf_op jit(solution)/shard_map/ppermute | solution.py:73
  5.0 1.0 %collective-permute-start.2 = (bf16[256,384]{1,0:T(8,128)(2,1)}, bf16[256,384]{1,0:T(8,128)(2,1)S(1)}, u32[]{:S(2)}, u32[]{:S(2)}) collective-permute-start(bf16[256,384]{1,0:T(8,128)(2,1)} %param.7), channel_id=1, source_target_pairs={{0,64},{64,128},{128,192},{192,0},{1,65},{65,129},{129,193},{193,1... | collective-permute-start | bytes 589832 | tf_op jit(solution)/shard_map/ppermute | solution.py:73
  6.0 0.7 fusion.38
  6.7 0.0 copy-done
  6.7 0.0 copy-start.5
  6.7 0.0 copy-start.6
  6.7 0.6 gather_fusion.1
  7.3 0.0 copy-start.4
  7.4 1.8 %gather_fusion = bf16[16,384,16]{1,2,0:T(8,128)(2,1)S(1)} fusion(bf16[64,384,16]{1,2,0:T(8,128)(2,1)} %param.10, s32[1024]{0:T(1024)S(1)} %pad_clamp_fusion), kind=kCustom, calls=%fused_computation | custom fusion | bytes 393280 | tf_op jit(solution)/shard_map/jit(_take)/gather | solution.py:117
  9.1 0.1 broadcast_select_fusion
  9.2 0.1 select_bitcast_fusion
  9.3 0.8 pad_maximum_fusion.1
  10.1 8.6 %all-to-all-start = ((bf16[16,32,384]{2,1,0:T(8,128)(2,1)}), bf16[16,32,384]{2,1,0:T(8,128)(2,1)}, u32[]{:S(2)}, u32[]{:S(2)}) async-start(bf16[16,32,384]{2,1,0:T(8,128)(2,1)} %pad_maximum_fusion.1), calls=%async_computation | async-start | bytes 786432 | tf_op jit(solution)/shard_map/all_to_all | solution.py:120
  18.7 0.0 copy-done.3
  18.8 0.0 copy-done.5
  18.8 0.7 fusion.54
  20.3 0.1 subtract_reduce_fusion
  20.4 0.1 convert_reduce_fusion
  20.5 0.1 dynamic_slice.60
  20.6 0.1 select_reduce_fusion
  20.9 0.0 collective-permute-done
  20.9 0.0 collective-permute-done.1
  21.0 0.0 collective-permute-done.2
  21.0 0.0 copy-start.1
  21.0 0.9 %copy-done.1 = bf16[1024,384]{1,0:T(8,128)(2,1)} copy-done((bf16[1024,384]{1,0:T(8,128)(2,1)}, bf16[1024,384]{1,0:T(8,128)(2,1)S(1)}, u32[]{:S(2)}) %copy-start.1) | copy-done | bytes 786456
  21.9 2.1 %fusion.17 = f32[1024,640]{0,1:T(8,128)S(1)} fusion(bf16[1024,384]{1,0:T(8,128)(2,1)} %copy-done.1, bf16[384,128]{1,0:T(8,128)(2,1)S(1)} %get-tuple-element.12, bf16[384,128]{1,0:T(8,128)(2,1)S(1)} %get-tuple-element.11, bf16[384,384]{1,0:T(8,128)(2,1)} %param.8), kind=kOutput, calls=%fused_computation.19 | convolution fusion | flops 504791040 | bytes 3899392 | tf_op jit(solution)/shard_map/dot_general | solution.py:145
  24.0 1.4 %constant_dynamic-slice_fusion.6 = (f32[256,640]{0,1:T(8,128)}, f32[256,640]{0,1:T(8,128)}, f32[256,640]{0,1:T(8,128)}) fusion(f32[1024,640]{0,1:T(8,128)S(1)} %fusion.17, s32[]{:T(128)S(6)} %select_n.159, s32[]{:T(128)S(6)} %select_n.163, s32[]{:T(128)S(6)} %select_n.161), kind=kLoop, calls=%fused_computation.74 | loop fusion | bytes 3932172 | tf_op jit(solution)/shard_map/dynamic_slice | solution.py:84
  25.4 1.5 %collective-permute-start.3 = (f32[256,640]{0,1:T(8,128)}, f32[256,640]{0,1:T(8,128)}, u32[]{:S(2)}, u32[]{:S(2)}) collective-permute-start(f32[256,640]{0,1:T(8,128)} %get-tuple-element.8), channel_id=1, source_target_pairs={{0,16},{16,32},{32,48},{48,0},{1,17},{17,33},{33,49},{49,1},{2,18}... | collective-permute-start | bytes 1966088 | tf_op jit(solution)/shard_map/ppermute | solution.py:85
  26.8 1.8 %collective-permute-start.5 = (f32[256,640]{0,1:T(8,128)}, f32[256,640]{0,1:T(8,128)}, u32[]{:S(2)}, u32[]{:S(2)}) collective-permute-start(f32[256,640]{0,1:T(8,128)} %get-tuple-element.9), channel_id=1, source_target_pairs={{0,48},{16,0},{32,16},{48,32},{1,49},{17,1},{33,17},{49,33},{2,50}... | collective-permute-start | bytes 1966088 | tf_op jit(solution)/shard_map/ppermute | solution.py:85
  28.6 1.8 %collective-permute-start.4 = (f32[256,640]{0,1:T(8,128)}, f32[256,640]{0,1:T(8,128)}, u32[]{:S(2)}, u32[]{:S(2)}) collective-permute-start(f32[256,640]{0,1:T(8,128)} %get-tuple-element.10), channel_id=1, source_target_pairs={{0,32},{16,48},{32,0},{48,16},{1,33},{17,49},{33,1},{49,17},{2,34}... | collective-permute-start | bytes 1966088 | tf_op jit(solution)/shard_map/ppermute | solution.py:85
  30.4 0.3 all-to-all-done
  30.8 1.6 %fusion.6 = f32[1024,16]{0,1:T(8,128)S(1)} fusion(bf16[1024,384]{1,0:T(8,128)(2,1)} %copy-done.1, pred[1024,16]{0,1:T(8,128)(4,1)S(1)} %iota_compare_fusion, bf16[16,32,384]{2,1,0:T(8,128)(2,1)} %all-to-all-done), kind=kOutput, calls=%fused_computation.10 | convolution fusion | flops 201834496 | bytes 1064960 | tf_op jit(solution)/shard_map/dot_general | solution.py:123
  32.4 1.6 %collective-permute-start.9 = (f32[256,16]{0,1:T(8,128)S(1)}, f32[256,16]{0,1:T(8,128)S(1)}, u32[]{:S(2)}, u32[]{:S(2)}) collective-permute-start(f32[256,16]{0,1:T(8,128)S(1)} %get-tuple-element.19), channel_id=1, source_target_pairs={{0,16},{16,32},{32,48},{48,0},{1,17},{17,33},{33,49},{49,1},{2,18}... | collective-permute-start | bytes 49160 | tf_op jit(solution)/shard_map/ppermute | solution.py:85
  34.0 1.5 %or_and_fusion = pred[256,1024]{0,1:T(8,128)(4,1)} fusion(s32[256]{0:T(256)S(1)} %dynamic_slice.60, s32[256]{0:T(256)S(1)} %iota_add_fusion, s32[1024]{0:T(1024)S(1)} %bitcast.61, s32[1024]{0:T(1024)S(1)} %bitcast.62, pred[1024]{0:T(1024)(128)(4,1)S(1)} %broadcast_compare_fusion), kind=kLoop, calls=%fused_computation.13 | loop fusion | flops 1048576 | bytes 273408 | tf_op jit(solution)/shard_map/and | solution.py:44
  35.5 0.1 dynamic-slice
  35.6 1.8 %collective-permute-start.11 = (f32[256,16]{0,1:T(8,128)S(1)}, f32[256,16]{0,1:T(8,128)S(1)}, u32[]{:S(2)}, u32[]{:S(2)}) collective-permute-start(f32[256,16]{0,1:T(8,128)S(1)} %get-tuple-element.20), channel_id=1, source_target_pairs={{0,48},{16,0},{32,16},{48,32},{1,49},{17,1},{33,17},{49,33},{2,50}... | collective-permute-start | bytes 49160 | tf_op jit(solution)/shard_map/ppermute | solution.py:85
  37.3 18.5 %collective-permute-done.9 = f32[256,16]{0,1:T(8,128)S(1)} collective-permute-done((f32[256,16]{0,1:T(8,128)S(1)}, f32[256,16]{0,1:T(8,128)S(1)}, u32[]{:S(2)}, u32[]{:S(2)}) %collective-permute-start.9) | collective-permute-done | bytes 16416 | tf_op jit(solution)/shard_map/ppermute | solution.py:85
  55.8 4.0 %collective-permute-start.10 = (f32[256,16]{0,1:T(8,128)S(1)}, f32[256,16]{0,1:T(8,128)}, u32[]{:S(2)}, u32[]{:S(2)}) collective-permute-start(f32[256,16]{0,1:T(8,128)S(1)} %get-tuple-element.21), channel_id=1, source_target_pairs={{0,32},{16,48},{32,0},{48,16},{1,33},{17,49},{33,1},{49,17},{2,34}... | collective-permute-start | bytes 49160 | tf_op jit(solution)/shard_map/ppermute | solution.py:85
  59.8 0.0 collective-permute-done.11
  59.8 1.8 %collective-permute-done.10 = f32[256,16]{0,1:T(8,128)} collective-permute-done((f32[256,16]{0,1:T(8,128)S(1)}, f32[256,16]{0,1:T(8,128)}, u32[]{:S(2)}, u32[]{:S(2)}) %collective-permute-start.10) | collective-permute-done | bytes 16416 | tf_op jit(solution)/shard_map/ppermute | solution.py:85
  61.6 0.7 add_add_fusion.1
  62.3 0.0 collective-permute-done.3
  62.3 0.0 collective-permute-done.5
  62.3 0.0 collective-permute-done.4
  62.3 1.7 %add_add_fusion = f32[256,640]{0,1:T(8,128)S(1)} fusion(f32[256,640]{0,1:T(8,128)} %collective-permute-done.5, f32[256,640]{0,1:T(8,128)} %collective-permute-done.4, f32[256,640]{0,1:T(8,128)} %collective-permute-done.3, f32[1024,640]{0,1:T(8,128)S(1)} %fusion.17, s32[]{:T(128)S(6)} %select_n.157), kind=kLoop, calls=%fused_computation.17 | loop fusion | flops 491520 | bytes 3276804 | tf_op jit(solution)/shard_map/add | solution.py:85
  64.0 2.2 %collective-permute-start.8 = (bf16[256,256]{0,1:T(8,128)(2,1)S(1)}, bf16[256,256]{0,1:T(8,128)(2,1)S(1)}, u32[]{:S(2)}, u32[]{:S(2)}) collective-permute-start(bf16[256,256]{0,1:T(8,128)(2,1)S(1)} %slice.53), channel_id=1, source_target_pairs={{0,16},{16,32},{32,48},{48,0},{1,17},{17,33},{33,49},{49,1},{2,18}... | collective-permute-start | bytes 393224 | tf_op jit(solution)/shard_map/ppermute | solution.py:73
  66.2 2.7 %collective-permute-start.7 = (bf16[256,256]{0,1:T(8,128)(2,1)S(1)}, bf16[256,256]{0,1:T(8,128)(2,1)S(1)}, u32[]{:S(2)}, u32[]{:S(2)}) collective-permute-start(bf16[256,256]{0,1:T(8,128)(2,1)S(1)} %slice.53), channel_id=1, source_target_pairs={{0,32},{16,48},{32,0},{48,16},{1,33},{17,49},{33,1},{49,17},{2,34}... | collective-permute-start | bytes 393224 | tf_op jit(solution)/shard_map/ppermute | solution.py:73
  68.9 1.4 %collective-permute-start.6 = (bf16[256,256]{0,1:T(8,128)(2,1)S(1)}, bf16[256,256]{0,1:T(8,128)(2,1)S(1)}, u32[]{:S(2)}, u32[]{:S(2)}) collective-permute-start(bf16[256,256]{0,1:T(8,128)(2,1)S(1)} %slice.53), channel_id=1, source_target_pairs={{0,48},{16,0},{32,16},{48,32},{1,49},{17,1},{33,17},{49,33},{2,50}... | collective-permute-start | bytes 393224 | tf_op jit(solution)/shard_map/ppermute | solution.py:73
  70.3 0.7 collective-permute-start.12
  71.0 1.3 %fusion.23 = bf16[256,384]{0,1:T(8,128)(2,1)S(1)} fusion(f32[256,640]{0,1:T(8,128)S(1)} %add_add_fusion, bf16[16,32,384]{2,1,0:T(8,128)(2,1)} %all-to-all-done, f32[256,16]{0,1:T(8,128)S(1)} %add_add_fusion.1, pred[256,16]{0,1:T(8,128)(4,1)S(1)} %iota_compare_fusion.2), kind=kOutput, calls=%fused_computation.26 | convolution fusion | flops 302252032 | bytes 806912 | tf_op jit(solution)/shard_map/dot_general | solution.py:141
  72.3 4.4 %collective-permute-done.12 = bf16[256,256]{0,1:T(8,128)(2,1)S(1)} collective-permute-done((bf16[256,256]{0,1:T(8,128)(2,1)S(1)}, bf16[256,256]{0,1:T(8,128)(2,1)S(1)}, u32[]{:S(2)}, u32[]{:S(2)}) %collective-permute-start.12) | collective-permute-done | bytes 131104 | tf_op jit(solution)/shard_map/ppermute | solution.py:150
  76.8 0.0 copy-start.2
  76.9 0.8 %copy.20 = bf16[256,512]{1,0:T(8,128)(2,1)} copy(bf16[256,512]{0,1:T(8,128)(2,1)S(1)} %pad_maximum_fusion.2) | data formatting | bytes 524288
  77.7 0.0 collective-permute-done.8
  77.7 0.0 collective-permute-done.7
  77.7 0.0 collective-permute-done.6
  77.7 0.1 pad_maximum_fusion
  77.8 1.7 %fusion = (f32[3,256]{1,0:T(4,128)S(1)}, f32[1024,256,3]{1,0,2:T(8,128)S(1)}) fusion(pred[256,1024]{0,1:T(8,128)(4,1)} %or_and_fusion, bf16[256,3,128]{0,2,1:T(8,128)(2,1)S(1)} %bitcast.59, bf16[1024,256]{0,1:T(8,128)(2,1)S(1)} %pad_maximum_fusion), kind=kOutput, calls=%fused_computation.4 | convolution fusion | flops 203685120 | bytes 3869696 | tf_op jit(solution)/shard_map/qhd,kd->hqk/dot_general | solution.py:48
  79.5 0.8 fusion.1
  80.3 1.0 %fusion.13 = bf16[256,3,128]{0,2,1:T(8,128)(2,1)S(1)} fusion(f32[1024,256,3]{1,0,2:T(8,128)S(1)} %get-tuple-element.23, f32[3,256]{1,0:T(4,128)S(1)} %broadcast_maximum_fusion, pred[256,1024]{0,1:T(8,128)(4,1)S(1)} %copy-done.2, bf16[1024,256]{0,1:T(8,128)(2,1)S(1)} %pad_maximum_fusion, f32[256,3]{0,1:T(4,128)S(1)} %bitcast.64), kind=kOutput, calls=%fused_computation.15 | convolution fusion | flops 205455360 | bytes 3874816 | tf_op jit(solution)/shard_map/hqk,kd->hqd/dot_general | solution.py:55
  81.3 0.8 copy.19
  (33 shorter events, 0.4 us)
Async XLA Ops:
  0.6 6.1 %copy-start = (bf16[64,16,384]{2,1,0:T(8,128)(2,1)S(1)}, bf16[64,16,384]{2,1,0:T(8,128)(2,1)}, u32[]{:S(2)}) copy-start(bf16[64,16,384]{2,1,0:T(8,128)(2,1)} %param.11) | copy-start | bytes 2359300
  0.6 18.1 %copy-start.3 = (bf16[256,384]{1,0:T(8,128)(2,1)S(1)}, bf16[256,384]{1,0:T(8,128)(2,1)}, u32[]{:S(2)}) copy-start(bf16[256,384]{1,0:T(8,128)(2,1)} %param.7) | copy-start | bytes 589828
  0.7 20.3 %collective-permute-start.1 = (bf16[256,384]{1,0:T(8,128)(2,1)}, bf16[256,384]{1,0:T(8,128)(2,1)S(1)}, u32[]{:S(2)}, u32[]{:S(2)}) collective-permute-start(bf16[256,384]{1,0:T(8,128)(2,1)} %param.7), channel_id=1, source_target_pairs={{0,128},{64,192},{128,0},{192,64},{1,129},{65,193},{129,1},{193,65... | collective-permute-start | bytes 589832 | tf_op jit(solution)/shard_map/ppermute | solution.py:73
  3.9 16.9 %collective-permute-start = (bf16[256,384]{1,0:T(8,128)(2,1)}, bf16[256,384]{1,0:T(8,128)(2,1)S(1)}, u32[]{:S(2)}, u32[]{:S(2)}) collective-permute-start(bf16[256,384]{1,0:T(8,128)(2,1)} %param.7), channel_id=1, source_target_pairs={{0,192},{64,0},{128,64},{192,128},{1,193},{65,1},{129,65},{193,129... | collective-permute-start | bytes 589832 | tf_op jit(solution)/shard_map/ppermute | solution.py:73
  5.0 16.0 %collective-permute-start.2 = (bf16[256,384]{1,0:T(8,128)(2,1)}, bf16[256,384]{1,0:T(8,128)(2,1)S(1)}, u32[]{:S(2)}, u32[]{:S(2)}) collective-permute-start(bf16[256,384]{1,0:T(8,128)(2,1)} %param.7), channel_id=1, source_target_pairs={{0,64},{64,128},{128,192},{192,0},{1,65},{65,129},{129,193},{193,1... | collective-permute-start | bytes 589832 | tf_op jit(solution)/shard_map/ppermute | solution.py:73
  6.7 12.1 %copy-start.5 = (s32[16,8]{0,1:T(8,128)S(1)}, s32[16,8]{0,1:T(8,128)}, u32[]{:S(2)}) copy-start(s32[16,8]{0,1:T(8,128)} %param.13) | copy-start | bytes 1540
  6.7 12.1 %copy-start.6 = (s32[16,8]{0,1:T(8,128)S(1)}, s32[16,8]{0,1:T(8,128)}, u32[]{:S(2)}) copy-start(s32[16,8]{0,1:T(8,128)} %param.12) | copy-start | bytes 1540
  7.3 13.5 %copy-start.4 = (bf16[384,512]{1,0:T(8,128)(2,1)S(1)}, bf16[384,512]{1,0:T(8,128)(2,1)}, u32[]{:S(2)}) copy-start(bf16[384,512]{1,0:T(8,128)(2,1)} %param.9) | copy-start | bytes 1179652
  10.1 20.6 %all-to-all-start = ((bf16[16,32,384]{2,1,0:T(8,128)(2,1)}), bf16[16,32,384]{2,1,0:T(8,128)(2,1)}, u32[]{:S(2)}, u32[]{:S(2)}) async-start(bf16[16,32,384]{2,1,0:T(8,128)(2,1)} %pad_maximum_fusion.1), calls=%async_computation | async-start | bytes 786432 | tf_op jit(solution)/shard_map/all_to_all | solution.py:120
  21.0 0.9 %copy-start.1 = (bf16[1024,384]{1,0:T(8,128)(2,1)}, bf16[1024,384]{1,0:T(8,128)(2,1)S(1)}, u32[]{:S(2)}) copy-start(bf16[1024,384]{1,0:T(8,128)(2,1)S(1)} %constant_dynamic-update-slice_fusion) | copy-start | bytes 2359300
  25.4 36.9 %collective-permute-start.3 = (f32[256,640]{0,1:T(8,128)}, f32[256,640]{0,1:T(8,128)}, u32[]{:S(2)}, u32[]{:S(2)}) collective-permute-start(f32[256,640]{0,1:T(8,128)} %get-tuple-element.8), channel_id=1, source_target_pairs={{0,16},{16,32},{32,48},{48,0},{1,17},{17,33},{33,49},{49,1},{2,18}... | collective-permute-start | bytes 1966088 | tf_op jit(solution)/shard_map/ppermute | solution.py:85
  26.8 35.5 %collective-permute-start.5 = (f32[256,640]{0,1:T(8,128)}, f32[256,640]{0,1:T(8,128)}, u32[]{:S(2)}, u32[]{:S(2)}) collective-permute-start(f32[256,640]{0,1:T(8,128)} %get-tuple-element.9), channel_id=1, source_target_pairs={{0,48},{16,0},{32,16},{48,32},{1,49},{17,1},{33,17},{49,33},{2,50}... | collective-permute-start | bytes 1966088 | tf_op jit(solution)/shard_map/ppermute | solution.py:85
  28.6 33.7 %collective-permute-start.4 = (f32[256,640]{0,1:T(8,128)}, f32[256,640]{0,1:T(8,128)}, u32[]{:S(2)}, u32[]{:S(2)}) collective-permute-start(f32[256,640]{0,1:T(8,128)} %get-tuple-element.10), channel_id=1, source_target_pairs={{0,32},{16,48},{32,0},{48,16},{1,33},{17,49},{33,1},{49,17},{2,34}... | collective-permute-start | bytes 1966088 | tf_op jit(solution)/shard_map/ppermute | solution.py:85
  32.4 23.4 %collective-permute-start.9 = (f32[256,16]{0,1:T(8,128)S(1)}, f32[256,16]{0,1:T(8,128)S(1)}, u32[]{:S(2)}, u32[]{:S(2)}) collective-permute-start(f32[256,16]{0,1:T(8,128)S(1)} %get-tuple-element.19), channel_id=1, source_target_pairs={{0,16},{16,32},{32,48},{48,0},{1,17},{17,33},{33,49},{49,1},{2,18}... | collective-permute-start | bytes 49160 | tf_op jit(solution)/shard_map/ppermute | solution.py:85
  35.6 24.2 %collective-permute-start.11 = (f32[256,16]{0,1:T(8,128)S(1)}, f32[256,16]{0,1:T(8,128)S(1)}, u32[]{:S(2)}, u32[]{:S(2)}) collective-permute-start(f32[256,16]{0,1:T(8,128)S(1)} %get-tuple-element.20), channel_id=1, source_target_pairs={{0,48},{16,0},{32,16},{48,32},{1,49},{17,1},{33,17},{49,33},{2,50}... | collective-permute-start | bytes 49160 | tf_op jit(solution)/shard_map/ppermute | solution.py:85
  55.8 5.8 %collective-permute-start.10 = (f32[256,16]{0,1:T(8,128)S(1)}, f32[256,16]{0,1:T(8,128)}, u32[]{:S(2)}, u32[]{:S(2)}) collective-permute-start(f32[256,16]{0,1:T(8,128)S(1)} %get-tuple-element.21), channel_id=1, source_target_pairs={{0,32},{16,48},{32,0},{48,16},{1,33},{17,49},{33,1},{49,17},{2,34}... | collective-permute-start | bytes 49160 | tf_op jit(solution)/shard_map/ppermute | solution.py:85
  64.0 13.7 %collective-permute-start.8 = (bf16[256,256]{0,1:T(8,128)(2,1)S(1)}, bf16[256,256]{0,1:T(8,128)(2,1)S(1)}, u32[]{:S(2)}, u32[]{:S(2)}) collective-permute-start(bf16[256,256]{0,1:T(8,128)(2,1)S(1)} %slice.53), channel_id=1, source_target_pairs={{0,16},{16,32},{32,48},{48,0},{1,17},{17,33},{33,49},{49,1},{2,18}... | collective-permute-start | bytes 393224 | tf_op jit(solution)/shard_map/ppermute | solution.py:73
  66.2 11.5 %collective-permute-start.7 = (bf16[256,256]{0,1:T(8,128)(2,1)S(1)}, bf16[256,256]{0,1:T(8,128)(2,1)S(1)}, u32[]{:S(2)}, u32[]{:S(2)}) collective-permute-start(bf16[256,256]{0,1:T(8,128)(2,1)S(1)} %slice.53), channel_id=1, source_target_pairs={{0,32},{16,48},{32,0},{48,16},{1,33},{17,49},{33,1},{49,17},{2,34}... | collective-permute-start | bytes 393224 | tf_op jit(solution)/shard_map/ppermute | solution.py:73
  68.9 8.8 %collective-permute-start.6 = (bf16[256,256]{0,1:T(8,128)(2,1)S(1)}, bf16[256,256]{0,1:T(8,128)(2,1)S(1)}, u32[]{:S(2)}, u32[]{:S(2)}) collective-permute-start(bf16[256,256]{0,1:T(8,128)(2,1)S(1)} %slice.53), channel_id=1, source_target_pairs={{0,48},{16,0},{32,16},{48,32},{1,49},{17,1},{33,17},{49,33},{2,50}... | collective-permute-start | bytes 393224 | tf_op jit(solution)/shard_map/ppermute | solution.py:73
  70.3 6.5 %collective-permute-start.12 = (bf16[256,256]{0,1:T(8,128)(2,1)S(1)}, bf16[256,256]{0,1:T(8,128)(2,1)S(1)}, u32[]{:S(2)}, u32[]{:S(2)}) collective-permute-start(bf16[256,256]{0,1:T(8,128)(2,1)S(1)} %slice.53), channel_id=1, source_target_pairs={{0,128},{64,192},{128,0},{192,64},{1,129},{65,193},{129,1},{193,65... | collective-permute-start | bytes 393224 | tf_op jit(solution)/shard_map/ppermute | solution.py:150
  76.8 2.7 %copy-start.2 = (pred[256,1024]{0,1:T(8,128)(4,1)S(1)}, pred[256,1024]{0,1:T(8,128)(4,1)}, u32[]{:S(2)}) copy-start(pred[256,1024]{0,1:T(8,128)(4,1)} %or_and_fusion) | copy-start | bytes 786436

commit v2 on v1

--- a/solution.py
+++ b/solution.py
@@ -34,15 +34,9 @@
         block_size = key_block.shape[0]
         key_rows = lax.dynamic_slice_in_dim(key_block, kv_group * head_size, head_size, 1)
         values = lax.dynamic_slice_in_dim(key_block, kv_half + kv_group * head_size, head_size, 1)
-        parts = block_size // own_rows
-        blocks = jnp.arange(block_size, dtype=jnp.int32).reshape(parts, own_rows)
-        blocks = jnp.concatenate([blocks, blocks], axis=0)
-        key_pos = lax.dynamic_slice_in_dim(blocks, key_start, parts, 0).reshape(-1)
-        seg_blocks = segment.reshape(parts, own_rows)
-        seg_blocks = jnp.concatenate([seg_blocks, seg_blocks], axis=0)
-        key_seg = lax.dynamic_slice_in_dim(seg_blocks, key_start, parts, 0).reshape(-1)
+        key_pos = jnp.arange(block_size, dtype=jnp.int32)
         allowed = (key_pos[None, :] <= query_pos[:, None]) & (
-            (key_seg[None, :] == query_seg[:, None]) | (key_seg[None, :] == 0)
+            (segment[None, :] == query_seg[:, None]) | (segment[None, :] == 0)
         )
         scores = (
             jnp.einsum("qhd,kd->hqk", query_heads, key_rows, preferred_element_type=jnp.float32)
@@ -72,6 +66,18 @@
         perm = [(i, (i - shift) % size) for i in range(size)]
         copies.append(lax.ppermute(x, axis_name, perm))
     return copies
+
+
+def ring_gather(x, axis_name, axis):
+    size = lax.axis_size(axis_name)
+    me = lax.axis_index(axis_name)
+    copies = shifted_copies(x, axis_name)
+    doubled = jnp.stack(copies + copies, axis=0)
+    ordered = lax.dynamic_slice_in_dim(doubled, size - me, size, 0)
+    moved = jnp.moveaxis(ordered, 0, axis)
+    shape = list(x.shape)
+    shape[axis] = shape[axis] * size
+    return moved.reshape(shape)
 
 
 def ring_reduce_scatter(x, axis_name, origin=0):
@@ -147,8 +153,8 @@
     query_rows = (summed[:, :query_cols] + adapter_term).astype(jnp.bfloat16)
     head_kv = summed[:, query_cols:].astype(jnp.bfloat16)
     partner = [(i, (i + row_size // kv_heads) % row_size) for i in range(row_size)]
+    key_values = ring_gather(head_kv, "col", 0)
     other_kv = lax.ppermute(head_kv, "row", partner)
-    key_values = jnp.concatenate(shifted_copies(head_kv, "col"), axis=0)
     first_is_own = kv_group == 0
     low_head = jnp.where(first_is_own, head_kv, other_kv)
     high_head = jnp.where(first_is_own, other_kv, head_kv)
@@ -158,7 +164,7 @@
     )
     attend, initial = make_attend(query_rows, segment, first_row, 0, head_size, head_size)
     _, running_sum, running_out = attend(
-        initial, key_values, col_index
+        initial, key_values, jnp.int32(0)
     )
     attention = (running_out / running_sum[:, :, None]).astype(jnp.bfloat16)
     attention = jnp.transpose(attention, (1, 0, 2)).reshape(own_rows, query_cols)

time: 82.6 us -> 79.7 us (0.965)
  the two profiles are of different devices: /device:TPU:32 before, /device:TPU:8 now
where the time goes in v2:
time: 79.7 us; the launch traced here: 79.3 us
  starting transfers between devices  34 us (43%)
  waiting for transfers between devices  22.1 us (28%)
  other arithmetic  7.58 us (10%)
  local copies, waits for them, and re-layouts  7.02 us (9%)
  matrix products  6.74 us (8%)
  between operations  1.89 us (2%)
    ppermute x6, waiting for transfers between devices, ring_reduce_scatter(): total = total + lax.ppermute(piece, axis_name, perm)  18.9 us
    ppermute x6, starting transfers between devices, ring_reduce_scatter(): total = total + lax.ppermute(piece, axis_name, perm)  12.3 us
    ppermute x6, starting transfers between devices, shifted_copies(): copies.append(lax.ppermute(x, axis_name, perm))  10.6 us
    all_to_all x1, starting transfers between devices, body(): lax.all_to_all(outgoing, 'dp', split_axis=0, concat_axis=0, tiled=True)  8.61 us
    unnamed x27, local copies, waits for them, and re-layouts  2.75 us
    ppermute x1, starting transfers between devices, body(): other_kv = lax.ppermute(head_kv, 'row', partner)  2.54 us
    add x2, other arithmetic, ring_reduce_scatter(): total = total + lax.ppermute(piece, axis_name, perm)  2.46 us
    dot_general x1, matrix products, body(): jnp.dot(gathered, both_weights, preferred_element_type=jnp.float32)  2.09 us
  transfers between devices with their start and end apart: 14, of which 4 were waited for; matrix products, arithmetic and copies ran while one was open for 19% of the time, Pallas kernels for 0%

profile of v2, /device:TPU:8, one launch (start us, length us, event | category | flops | bytes accessed | tf_op | source)
XLA Modules:
  0.0 79.3 jit_solution(7379553747320196568)
XLA Ops:
  0.6 0.0 copy-start
  0.6 0.0 copy-start.3
  0.7 2.4 %collective-permute-start.1 = (bf16[256,384]{1,0:T(8,128)(2,1)}, bf16[256,384]{1,0:T(8,128)(2,1)S(1)}, u32[]{:S(2)}, u32[]{:S(2)}) collective-permute-start(bf16[256,384]{1,0:T(8,128)(2,1)} %param.7), channel_id=1, source_target_pairs={{0,128},{64,192},{128,0},{192,64},{1,129},{65,193},{129,1},{193,65... | collective-permute-start | bytes 589832 | tf_op jit(solution)/shard_map/ppermute | solution.py:67
  3.0 1.3 %collective-permute-start = (bf16[256,384]{1,0:T(8,128)(2,1)}, bf16[256,384]{1,0:T(8,128)(2,1)S(1)}, u32[]{:S(2)}, u32[]{:S(2)}) collective-permute-start(bf16[256,384]{1,0:T(8,128)(2,1)} %param.7), channel_id=1, source_target_pairs={{0,192},{64,0},{128,64},{192,128},{1,193},{65,1},{129,65},{193,129... | collective-permute-start | bytes 589832 | tf_op jit(solution)/shard_map/ppermute | solution.py:67
  4.4 0.7 collective-permute-start.2
  5.1 0.7 fusion.39
  5.8 0.0 copy-done
  5.8 0.0 copy-start.5
  5.8 0.0 copy-start.6
  5.8 0.6 gather_fusion.1
  6.4 0.0 copy-start.4
  6.5 1.8 %gather_fusion = bf16[16,384,16]{1,2,0:T(8,128)(2,1)S(1)} fusion(bf16[64,384,16]{1,2,0:T(8,128)(2,1)} %param.10, s32[1024]{0:T(1024)S(1)} %pad_clamp_fusion), kind=kCustom, calls=%fused_computation | custom fusion | bytes 393280 | tf_op jit(solution)/shard_map/jit(_take)/gather | solution.py:123
  8.2 0.1 broadcast_select_fusion
  8.3 0.1 select_bitcast_fusion
  8.4 0.8 %pad_maximum_fusion = bf16[16,32,384]{2,1,0:T(8,128)(2,1)} fusion(bf16[16,16,384]{2,1,0:T(8,128)(2,1)S(1)} %broadcast_select_fusion, bf16[16,16,384]{2,1,0:T(8,128)(2,1)S(1)} %select_bitcast_fusion), kind=kLoop, calls=%fused_computation.27 | loop fusion | flops 786432 | bytes 786432 | tf_op jit(solution)/shard_map/concatenate | solution.py:125
  9.2 8.6 %all-to-all-start = ((bf16[16,32,384]{2,1,0:T(8,128)(2,1)}), bf16[16,32,384]{2,1,0:T(8,128)(2,1)}, u32[]{:S(2)}, u32[]{:S(2)}) async-start(bf16[16,32,384]{2,1,0:T(8,128)(2,1)} %pad_maximum_fusion), calls=%async_computation | async-start | bytes 786432 | tf_op jit(solution)/shard_map/all_to_all | solution.py:126
  18.0 0.0 copy-done.3
  18.0 0.0 copy-done.5
  18.0 0.0 copy-done.6
  18.0 0.7 fusion.51
  19.5 0.1 subtract_reduce_fusion
  19.6 0.1 convert_reduce_fusion
  19.7 0.1 dynamic_slice.55
  19.8 0.1 select_reduce_fusion
  20.0 0.0 copy-done.4
  20.0 0.0 collective-permute-done
  20.1 0.0 collective-permute-done.1
  20.1 0.0 collective-permute-done.2
  20.2 0.9 %copy-done.1 = bf16[1024,384]{1,0:T(8,128)(2,1)} copy-done((bf16[1024,384]{1,0:T(8,128)(2,1)}, bf16[1024,384]{1,0:T(8,128)(2,1)S(1)}, u32[]{:S(2)}) %copy-start.1) | copy-done | bytes 786456
  21.1 2.1 %fusion.18 = f32[1024,640]{0,1:T(8,128)S(1)} fusion(bf16[1024,384]{1,0:T(8,128)(2,1)} %copy-done.1, bf16[384,128]{1,0:T(8,128)(2,1)S(1)} %get-tuple-element.16, bf16[384,128]{1,0:T(8,128)(2,1)S(1)} %get-tuple-element.15, bf16[384,384]{1,0:T(8,128)(2,1)} %param.8), kind=kOutput, calls=%fused_computation.19 | convolution fusion | flops 504791040 | bytes 3899392 | tf_op jit(solution)/shard_map/dot_general | solution.py:151
  23.2 1.4 %constant_dynamic-slice_fusion.6 = (f32[256,640]{0,1:T(8,128)}, f32[256,640]{0,1:T(8,128)}, f32[256,640]{0,1:T(8,128)}) fusion(f32[1024,640]{0,1:T(8,128)S(1)} %fusion.18, s32[]{:T(128)S(6)} %select_n.157, s32[]{:T(128)S(6)} %select_n.161, s32[]{:T(128)S(6)} %select_n.159), kind=kLoop, calls=%fused_computation.93 | loop fusion | bytes 3932172 | tf_op jit(solution)/shard_map/dynamic_slice | solution.py:90
  24.5 1.5 %collective-permute-start.3 = (f32[256,640]{0,1:T(8,128)}, f32[256,640]{0,1:T(8,128)}, u32[]{:S(2)}, u32[]{:S(2)}) collective-permute-start(f32[256,640]{0,1:T(8,128)} %get-tuple-element.12), channel_id=1, source_target_pairs={{0,16},{16,32},{32,48},{48,0},{1,17},{17,33},{33,49},{49,1},{2,18}... | collective-permute-start | bytes 1966088 | tf_op jit(solution)/shard_map/ppermute | solution.py:91
  26.0 1.8 %collective-permute-start.5 = (f32[256,640]{0,1:T(8,128)}, f32[256,640]{0,1:T(8,128)}, u32[]{:S(2)}, u32[]{:S(2)}) collective-permute-start(f32[256,640]{0,1:T(8,128)} %get-tuple-element.13), channel_id=1, source_target_pairs={{0,48},{16,0},{32,16},{48,32},{1,49},{17,1},{33,17},{49,33},{2,50}... | collective-permute-start | bytes 1966088 | tf_op jit(solution)/shard_map/ppermute | solution.py:91
  27.8 1.8 %collective-permute-start.4 = (f32[256,640]{0,1:T(8,128)}, f32[256,640]{0,1:T(8,128)}, u32[]{:S(2)}, u32[]{:S(2)}) collective-permute-start(f32[256,640]{0,1:T(8,128)} %get-tuple-element.14), channel_id=1, source_target_pairs={{0,32},{16,48},{32,0},{48,16},{1,33},{17,49},{33,1},{49,17},{2,34}... | collective-permute-start | bytes 1966088 | tf_op jit(solution)/shard_map/ppermute | solution.py:91
  29.6 2.0 %all-to-all-done = bf16[16,32,384]{2,1,0:T(8,128)(2,1)} async-done(((bf16[16,32,384]{2,1,0:T(8,128)(2,1)}), bf16[16,32,384]{2,1,0:T(8,128)(2,1)}, u32[]{:S(2)}, u32[]{:S(2)}) %all-to-all-start) | async-done | bytes 393248 | tf_op jit(solution)/shard_map/all_to_all | solution.py:126
  31.6 1.6 %fusion.6 = f32[1024,16]{0,1:T(8,128)S(1)} fusion(bf16[1024,384]{1,0:T(8,128)(2,1)} %copy-done.1, pred[1024,16]{0,1:T(8,128)(4,1)S(1)} %iota_compare_fusion.1, bf16[16,32,384]{2,1,0:T(8,128)(2,1)} %all-to-all-done), kind=kOutput, calls=%fused_computation.10 | convolution fusion | flops 201834496 | bytes 1064960 | tf_op jit(solution)/shard_map/dot_general | solution.py:129
  33.2 1.6 %collective-permute-start.9 = (f32[256,16]{0,1:T(8,128)S(1)}, f32[256,16]{0,1:T(8,128)S(1)}, u32[]{:S(2)}, u32[]{:S(2)}) collective-permute-start(f32[256,16]{0,1:T(8,128)S(1)} %get-tuple-element.23), channel_id=1, source_target_pairs={{0,16},{16,32},{32,48},{48,0},{1,17},{17,33},{33,49},{49,1},{2,18}... | collective-permute-start | bytes 49160 | tf_op jit(solution)/shard_map/ppermute | solution.py:91
  34.8 1.4 %fusion.10 = pred[256,1024]{0,1:T(8,128)(4,1)} fusion(s32[256]{0:T(256)S(1)} %dynamic_slice.55, s32[256]{0:T(256)S(1)} %iota_add_fusion, s32[1024]{0:T(1024)S(1)} %convert_reduce_fusion, pred[1024]{0:T(1024)(128)(4,1)S(1)} %broadcast_compare_fusion), kind=kLoop, calls=%fused_computation.14 | loop fusion | flops 1048576 | bytes 269312 | tf_op jit(solution)/shard_map/and | solution.py:38
  36.2 0.1 dynamic-slice
  36.3 1.8 %collective-permute-start.11 = (f32[256,16]{0,1:T(8,128)S(1)}, f32[256,16]{0,1:T(8,128)S(1)}, u32[]{:S(2)}, u32[]{:S(2)}) collective-permute-start(f32[256,16]{0,1:T(8,128)S(1)} %get-tuple-element.24), channel_id=1, source_target_pairs={{0,48},{16,0},{32,16},{48,32},{1,49},{17,1},{33,17},{49,33},{2,50}... | collective-permute-start | bytes 49160 | tf_op jit(solution)/shard_map/ppermute | solution.py:91
  38.0 17.1 %collective-permute-done.9 = f32[256,16]{0,1:T(8,128)S(1)} collective-permute-done((f32[256,16]{0,1:T(8,128)S(1)}, f32[256,16]{0,1:T(8,128)S(1)}, u32[]{:S(2)}, u32[]{:S(2)}) %collective-permute-start.9) | collective-permute-done | bytes 16416 | tf_op jit(solution)/shard_map/ppermute | solution.py:91
  55.1 4.0 %collective-permute-start.10 = (f32[256,16]{0,1:T(8,128)S(1)}, f32[256,16]{0,1:T(8,128)}, u32[]{:S(2)}, u32[]{:S(2)}) collective-permute-start(f32[256,16]{0,1:T(8,128)S(1)} %get-tuple-element.25), channel_id=1, source_target_pairs={{0,32},{16,48},{32,0},{48,16},{1,33},{17,49},{33,1},{49,17},{2,34}... | collective-permute-start | bytes 49160 | tf_op jit(solution)/shard_map/ppermute | solution.py:91
  59.1 0.0 collective-permute-done.11
  59.1 1.8 %collective-permute-done.10 = f32[256,16]{0,1:T(8,128)} collective-permute-done((f32[256,16]{0,1:T(8,128)S(1)}, f32[256,16]{0,1:T(8,128)}, u32[]{:S(2)}, u32[]{:S(2)}) %collective-permute-start.10) | collective-permute-done | bytes 16416 | tf_op jit(solution)/shard_map/ppermute | solution.py:91
  60.9 0.7 add_add_fusion.1
  61.6 0.0 collective-permute-done.3
  61.6 0.0 collective-permute-done.5
  61.6 0.0 collective-permute-done.4
  61.6 1.7 %add_add_fusion = f32[256,640]{0,1:T(8,128)S(1)} fusion(f32[256,640]{0,1:T(8,128)} %collective-permute-done.5, f32[256,640]{0,1:T(8,128)} %collective-permute-done.4, f32[256,640]{0,1:T(8,128)} %collective-permute-done.3, f32[1024,640]{0,1:T(8,128)S(1)} %fusion.18, s32[]{:T(128)S(6)} %select_n.155), kind=kLoop, calls=%fused_computation.18 | loop fusion | flops 491520 | bytes 3276804 | tf_op jit(solution)/shard_map/add | solution.py:91
  63.4 2.5 %collective-permute-start.12 = (bf16[256,256]{0,1:T(8,128)(2,1)S(1)}, bf16[256,256]{0,1:T(8,128)(2,1)S(1)}, u32[]{:S(2)}, u32[]{:S(2)}) collective-permute-start(bf16[256,256]{0,1:T(8,128)(2,1)S(1)} %get-tuple-element.9), channel_id=1, source_target_pairs={{0,128},{64,192},{128,0},{192,64},{1,129},{65,193},{129,1},{193,65... | collective-permute-start | bytes 393224 | tf_op jit(solution)/shard_map/ppermute | solution.py:157
  65.9 2.0 %collective-permute-start.8 = (bf16[256,256]{0,1:T(8,128)(2,1)S(1)}, bf16[256,256]{0,1:T(8,128)(2,1)S(1)}, u32[]{:S(2)}, u32[]{:S(2)}) collective-permute-start(bf16[256,256]{0,1:T(8,128)(2,1)S(1)} %get-tuple-element.9), channel_id=1, source_target_pairs={{0,16},{16,32},{32,48},{48,0},{1,17},{17,33},{33,49},{49,1},{2,18}... | collective-permute-start | bytes 393224 | tf_op jit(solution)/shard_map/ppermute | solution.py:67
  67.9 2.7 %collective-permute-start.7 = (bf16[256,256]{0,1:T(8,128)(2,1)S(1)}, bf16[256,256]{0,1:T(8,128)(2,1)S(1)}, u32[]{:S(2)}, u32[]{:S(2)}) collective-permute-start(bf16[256,256]{0,1:T(8,128)(2,1)S(1)} %get-tuple-element.9), channel_id=1, source_target_pairs={{0,32},{16,48},{32,0},{48,16},{1,33},{17,49},{33,1},{49,17},{2,34}... | collective-permute-start | bytes 393224 | tf_op jit(solution)/shard_map/ppermute | solution.py:67
  70.6 1.5 %collective-permute-start.6 = (bf16[256,256]{0,1:T(8,128)(2,1)S(1)}, bf16[256,256]{0,1:T(8,128)(2,1)S(1)}, u32[]{:S(2)}, u32[]{:S(2)}) collective-permute-start(bf16[256,256]{0,1:T(8,128)(2,1)S(1)} %get-tuple-element.9), channel_id=1, source_target_pairs={{0,48},{16,0},{32,16},{48,32},{1,49},{17,1},{33,17},{49,33},{2,50}... | collective-permute-start | bytes 393224 | tf_op jit(solution)/shard_map/ppermute | solution.py:67
  72.1 1.3 %fusion.24 = bf16[256,384]{0,1:T(8,128)(2,1)S(1)} fusion(f32[256,640]{0,1:T(8,128)S(1)} %add_add_fusion, bf16[16,32,384]{2,1,0:T(8,128)(2,1)} %all-to-all-done, f32[256,16]{0,1:T(8,128)S(1)} %add_add_fusion.1, pred[256,16]{0,1:T(8,128)(4,1)S(1)} %iota_compare_fusion.3), kind=kOutput, calls=%fused_computation.26 | convolution fusion | flops 302252032 | bytes 806912 | tf_op jit(solution)/shard_map/dot_general | solution.py:147
  73.4 0.0 collective-permute-done.12
  73.5 0.8 %copy.28 = bf16[256,512]{1,0:T(8,128)(2,1)} copy(bf16[256,512]{0,1:T(8,128)(2,1)S(1)} %pad_maximum_fusion.1) | data formatting | bytes 524288
  74.4 1.2 %collective-permute-done.6 = bf16[256,256]{0,1:T(8,128)(2,1)S(1)} collective-permute-done((bf16[256,256]{0,1:T(8,128)(2,1)S(1)}, bf16[256,256]{0,1:T(8,128)(2,1)S(1)}, u32[]{:S(2)}, u32[]{:S(2)}) %collective-permute-start.6) | collective-permute-done | bytes 131104 | tf_op jit(solution)/shard_map/ppermute | solution.py:67
  75.6 0.0 collective-permute-done.7
  75.6 0.0 collective-permute-done.8
  75.8 0.2 copy.22
  76.0 0.7 fusion
  76.7 0.8 %fusion.1 = f32[3,256]{1,0:T(4,128)S(1)} fusion(f32[1024,256,3]{1,0,2:T(8,128)S(1)} %get-tuple-element.27, f32[3,256]{1,0:T(4,128)S(1)} %broadcast_maximum_fusion, pred[256,1024]{0,1:T(8,128)(4,1)S(1)} %copy-done.2), kind=kLoop, calls=%fused_computation.5 | loop fusion | flops 3931392 | bytes 3414016 | tf_op jit(solution)/shard_map/reduce_sum | solution.py:48
  77.5 1.0 %fusion.14 = bf16[256,3,128]{0,2,1:T(8,128)(2,1)S(1)} fusion(f32[1024,256,3]{1,0,2:T(8,128)S(1)} %get-tuple-element.27, f32[3,256]{1,0:T(4,128)S(1)} %broadcast_maximum_fusion, pred[256,1024]{0,1:T(8,128)(4,1)S(1)} %copy-done.2, bf16[1024,256]{1,0:T(8,128)(2,1)S(1)} %bitcast.67, f32[256,3]{0,1:T(4,128)S(1)} %bitcast.71), kind=kOutput, calls=%fused_computation.16 | convolution fusion | flops 205455360 | bytes 3874816 | tf_op jit(solution)/shard_map/hqk,kd->hqd/dot_general | solution.py:49
  78.5 0.8 %copy.27 = bf16[256,384]{1,0:T(8,128)(2,1)} copy(bf16[256,384]{0,1:T(8,128)(2,1)S(1)} %bitcast.68) | data formatting | bytes 393216
  (35 shorter events, 0.5 us)
Async XLA Ops:
  0.6 5.2 %copy-start = (bf16[64,16,384]{2,1,0:T(8,128)(2,1)S(1)}, bf16[64,16,384]{2,1,0:T(8,128)(2,1)}, u32[]{:S(2)}) copy-start(bf16[64,16,384]{2,1,0:T(8,128)(2,1)} %param.11) | copy-start | bytes 2359300
  0.6 17.3 %copy-start.3 = (bf16[256,384]{1,0:T(8,128)(2,1)S(1)}, bf16[256,384]{1,0:T(8,128)(2,1)}, u32[]{:S(2)}) copy-start(bf16[256,384]{1,0:T(8,128)(2,1)} %param.7) | copy-start | bytes 589828
  0.7 19.4 %collective-permute-start.1 = (bf16[256,384]{1,0:T(8,128)(2,1)}, bf16[256,384]{1,0:T(8,128)(2,1)S(1)}, u32[]{:S(2)}, u32[]{:S(2)}) collective-permute-start(bf16[256,384]{1,0:T(8,128)(2,1)} %param.7), channel_id=1, source_target_pairs={{0,128},{64,192},{128,0},{192,64},{1,129},{65,193},{129,1},{193,65... | collective-permute-start | bytes 589832 | tf_op jit(solution)/shard_map/ppermute | solution.py:67
  3.0 17.0 %collective-permute-start = (bf16[256,384]{1,0:T(8,128)(2,1)}, bf16[256,384]{1,0:T(8,128)(2,1)S(1)}, u32[]{:S(2)}, u32[]{:S(2)}) collective-permute-start(bf16[256,384]{1,0:T(8,128)(2,1)} %param.7), channel_id=1, source_target_pairs={{0,192},{64,0},{128,64},{192,128},{1,193},{65,1},{129,65},{193,129... | collective-permute-start | bytes 589832 | tf_op jit(solution)/shard_map/ppermute | solution.py:67
  4.4 15.7 %collective-permute-start.2 = (bf16[256,384]{1,0:T(8,128)(2,1)}, bf16[256,384]{1,0:T(8,128)(2,1)S(1)}, u32[]{:S(2)}, u32[]{:S(2)}) collective-permute-start(bf16[256,384]{1,0:T(8,128)(2,1)} %param.7), channel_id=1, source_target_pairs={{0,64},{64,128},{128,192},{192,0},{1,65},{65,129},{129,193},{193,1... | collective-permute-start | bytes 589832 | tf_op jit(solution)/shard_map/ppermute | solution.py:67
  5.8 12.2 %copy-start.5 = (s32[16,8]{0,1:T(8,128)S(1)}, s32[16,8]{0,1:T(8,128)}, u32[]{:S(2)}) copy-start(s32[16,8]{0,1:T(8,128)} %param.13) | copy-start | bytes 1540
  5.8 12.2 %copy-start.6 = (s32[16,8]{0,1:T(8,128)S(1)}, s32[16,8]{0,1:T(8,128)}, u32[]{:S(2)}) copy-start(s32[16,8]{0,1:T(8,128)} %param.12) | copy-start | bytes 1540
  6.4 13.5 %copy-start.4 = (bf16[384,512]{1,0:T(8,128)(2,1)S(1)}, bf16[384,512]{1,0:T(8,128)(2,1)}, u32[]{:S(2)}) copy-start(bf16[384,512]{1,0:T(8,128)(2,1)} %param.9) | copy-start | bytes 1179652
  9.2 22.3 %all-to-all-start = ((bf16[16,32,384]{2,1,0:T(8,128)(2,1)}), bf16[16,32,384]{2,1,0:T(8,128)(2,1)}, u32[]{:S(2)}, u32[]{:S(2)}) async-start(bf16[16,32,384]{2,1,0:T(8,128)(2,1)} %pad_maximum_fusion), calls=%async_computation | async-start | bytes 786432 | tf_op jit(solution)/shard_map/all_to_all | solution.py:126
  20.2 0.9 %copy-start.1 = (bf16[1024,384]{1,0:T(8,128)(2,1)}, bf16[1024,384]{1,0:T(8,128)(2,1)S(1)}, u32[]{:S(2)}) copy-start(bf16[1024,384]{1,0:T(8,128)(2,1)S(1)} %constant_dynamic-update-slice_fusion) | copy-start | bytes 2359300
  24.5 37.1 %collective-permute-start.3 = (f32[256,640]{0,1:T(8,128)}, f32[256,640]{0,1:T(8,128)}, u32[]{:S(2)}, u32[]{:S(2)}) collective-permute-start(f32[256,640]{0,1:T(8,128)} %get-tuple-element.12), channel_id=1, source_target_pairs={{0,16},{16,32},{32,48},{48,0},{1,17},{17,33},{33,49},{49,1},{2,18}... | collective-permute-start | bytes 1966088 | tf_op jit(solution)/shard_map/ppermute | solution.py:91
  26.0 35.6 %collective-permute-start.5 = (f32[256,640]{0,1:T(8,128)}, f32[256,640]{0,1:T(8,128)}, u32[]{:S(2)}, u32[]{:S(2)}) collective-permute-start(f32[256,640]{0,1:T(8,128)} %get-tuple-element.13), channel_id=1, source_target_pairs={{0,48},{16,0},{32,16},{48,32},{1,49},{17,1},{33,17},{49,33},{2,50}... | collective-permute-start | bytes 1966088 | tf_op jit(solution)/shard_map/ppermute | solution.py:91
  27.8 33.9 %collective-permute-start.4 = (f32[256,640]{0,1:T(8,128)}, f32[256,640]{0,1:T(8,128)}, u32[]{:S(2)}, u32[]{:S(2)}) collective-permute-start(f32[256,640]{0,1:T(8,128)} %get-tuple-element.14), channel_id=1, source_target_pairs={{0,32},{16,48},{32,0},{48,16},{1,33},{17,49},{33,1},{49,17},{2,34}... | collective-permute-start | bytes 1966088 | tf_op jit(solution)/shard_map/ppermute | solution.py:91
  33.2 21.9 %collective-permute-start.9 = (f32[256,16]{0,1:T(8,128)S(1)}, f32[256,16]{0,1:T(8,128)S(1)}, u32[]{:S(2)}, u32[]{:S(2)}) collective-permute-start(f32[256,16]{0,1:T(8,128)S(1)} %get-tuple-element.23), channel_id=1, source_target_pairs={{0,16},{16,32},{32,48},{48,0},{1,17},{17,33},{33,49},{49,1},{2,18}... | collective-permute-start | bytes 49160 | tf_op jit(solution)/shard_map/ppermute | solution.py:91
  36.3 22.8 %collective-permute-start.11 = (f32[256,16]{0,1:T(8,128)S(1)}, f32[256,16]{0,1:T(8,128)S(1)}, u32[]{:S(2)}, u32[]{:S(2)}) collective-permute-start(f32[256,16]{0,1:T(8,128)S(1)} %get-tuple-element.24), channel_id=1, source_target_pairs={{0,48},{16,0},{32,16},{48,32},{1,49},{17,1},{33,17},{49,33},{2,50}... | collective-permute-start | bytes 49160 | tf_op jit(solution)/shard_map/ppermute | solution.py:91
  55.1 5.8 %collective-permute-start.10 = (f32[256,16]{0,1:T(8,128)S(1)}, f32[256,16]{0,1:T(8,128)}, u32[]{:S(2)}, u32[]{:S(2)}) collective-permute-start(f32[256,16]{0,1:T(8,128)S(1)} %get-tuple-element.25), channel_id=1, source_target_pairs={{0,32},{16,48},{32,0},{48,16},{1,33},{17,49},{33,1},{49,17},{2,34}... | collective-permute-start | bytes 49160 | tf_op jit(solution)/shard_map/ppermute | solution.py:91
  63.4 10.0 %collective-permute-start.12 = (bf16[256,256]{0,1:T(8,128)(2,1)S(1)}, bf16[256,256]{0,1:T(8,128)(2,1)S(1)}, u32[]{:S(2)}, u32[]{:S(2)}) collective-permute-start(bf16[256,256]{0,1:T(8,128)(2,1)S(1)} %get-tuple-element.9), channel_id=1, source_target_pairs={{0,128},{64,192},{128,0},{192,64},{1,129},{65,193},{129,1},{193,65... | collective-permute-start | bytes 393224 | tf_op jit(solution)/shard_map/ppermute | solution.py:157
  65.9 9.7 %collective-permute-start.8 = (bf16[256,256]{0,1:T(8,128)(2,1)S(1)}, bf16[256,256]{0,1:T(8,128)(2,1)S(1)}, u32[]{:S(2)}, u32[]{:S(2)}) collective-permute-start(bf16[256,256]{0,1:T(8,128)(2,1)S(1)} %get-tuple-element.9), channel_id=1, source_target_pairs={{0,16},{16,32},{32,48},{48,0},{1,17},{17,33},{33,49},{49,1},{2,18}... | collective-permute-start | bytes 393224 | tf_op jit(solution)/shard_map/ppermute | solution.py:67
  67.9 7.7 %collective-permute-start.7 = (bf16[256,256]{0,1:T(8,128)(2,1)S(1)}, bf16[256,256]{0,1:T(8,128)(2,1)S(1)}, u32[]{:S(2)}, u32[]{:S(2)}) collective-permute-start(bf16[256,256]{0,1:T(8,128)(2,1)S(1)} %get-tuple-element.9), channel_id=1, source_target_pairs={{0,32},{16,48},{32,0},{48,16},{1,33},{17,49},{33,1},{49,17},{2,34}... | collective-permute-start | bytes 393224 | tf_op jit(solution)/shard_map/ppermute | solution.py:67
  70.6 5.0 %collective-permute-start.6 = (bf16[256,256]{0,1:T(8,128)(2,1)S(1)}, bf16[256,256]{0,1:T(8,128)(2,1)S(1)}, u32[]{:S(2)}, u32[]{:S(2)}) collective-permute-start(bf16[256,256]{0,1:T(8,128)(2,1)S(1)} %get-tuple-element.9), channel_id=1, source_target_pairs={{0,48},{16,0},{32,16},{48,32},{1,49},{17,1},{33,17},{49,33},{2,50}... | collective-permute-start | bytes 393224 | tf_op jit(solution)/shard_map/ppermute | solution.py:67
  73.4 2.6 %copy-start.2 = (pred[256,1024]{0,1:T(8,128)(4,1)S(1)}, pred[256,1024]{0,1:T(8,128)(4,1)}, u32[]{:S(2)}) copy-start(pred[256,1024]{0,1:T(8,128)(4,1)} %fusion.10) | copy-start | bytes 786436
